TPU v7x, 32 devices: a whole 2x2x4 slice. The times are simulated.
32 devices in a mesh: row: 4 (over y, core), col: 8 (over z, x).
Axes of the slice: x: 2, y: 2, z: 4, core: 2. Of those that a mesh axis runs over, the one named last changes fastest.
Arguments:
- hess: bfloat16 [10, 4, 256, 5, 8, 256], P(None, 'row', None, None, 'col'), may hold values from -6 to 6
- coupling: float32 [32, 256, 2, 256], P(('row', 'col')), may hold values from -6 to 6
- dest_row: int32 [32, 256, 1], P(('row', 'col')), may hold values from 0 to 3, as said below
- local_row: int32 [32, 256], P(('row', 'col')), may hold values from 256 to 2559
- live: int32 [32], P(('row', 'col')), may hold values from 1 to 256, 6144 in all
- pattern: int32 [40, 40], replicated, may hold values 0 or 1
Outputs:
- factor: float32 [10, 4, 256, 5, 8, 256], P(None, 'row', None, None, 'col')
Inputs may be any that keep to these rules, and one draw needn't show every extreme that they name: `dest_row`: among one owner's 256 slots, used or not, one grid row is named exactly 64 times and no grid row more than 64 times. The first live[d] slots of owner d are used; the counts sum to 6144 and one owner uses all 256.
All inputs are finite; a program needn't handle non-finite values. No bound on the sum of `live` on one device may be relied on, other than what follows from the above.
Results may differ from a plain program's by a relative error of at most 0.0003.
Values sent between devices are 32-bit elements; how exact they have to be, the bound alone decides.
No kernel may reach another device: no remote copies, remote signals or barrier semaphores. Data moves between devices by JAX's collectives and lax.ppermute only.
A program may use at most 192 MiB of HBM per device.

v0:
```python
import jax
import jax.numpy as jnp
from jax import lax
from jax.sharding import PartitionSpec as P


def broadcast(value, axis, source):
    kept = jnp.where(lax.axis_index(axis) == source, value, 0).astype(value.dtype)
    return lax.psum(kept, axis)


def symmetric(block):
    return jnp.tril(block) + jnp.swapaxes(jnp.tril(block, -1), -1, -2)


def right_solve(rows, lower_factor):
    return jax.scipy.linalg.solve_triangular(lower_factor, rows.T, lower=True).T


def leading(block00, block10, block11, link):
    size = block00.shape[0]
    first = symmetric(block00)
    second = symmetric(block11)
    coupled = link * block10
    whole = jnp.concatenate(
        [jnp.concatenate([first, coupled.T], 1), jnp.concatenate([coupled, second], 1)], 0
    )
    ident = jnp.eye(2 * size, dtype=whole.dtype)
    spread = jnp.sum(jnp.abs(whole), axis=1) - jnp.abs(jnp.diagonal(whole))
    whole = whole * (1.0 - ident) + ident * (1.0 + spread)[:, None]
    factor00 = jnp.linalg.cholesky(whole[:size, :size])
    factor10 = right_solve(whole[size:, :size], factor00)
    reduced = whole[size:, size:] - jnp.dot(factor10, factor10.T, precision=lax.Precision.HIGHEST)
    factor11 = jnp.linalg.cholesky(reduced)
    return (factor00, factor10, factor11)


def solve_rows(rows, lower_factor):
    result = right_solve(rows, lower_factor)
    return result


def panel_solve(block_rows, f00, f10, f11):
    first = solve_rows(block_rows[:, 0], f00)
    second = solve_rows(
        block_rows[:, 1] - jnp.dot(first, f10.T, precision=lax.Precision.HIGHEST), f11
    )
    return jnp.stack([first, second], 1)


def shards(hess, coupling, dest_row, local_row, live, pattern):
    grid_rows = lax.axis_size("row")
    grid_cols = lax.axis_size("col")
    here_row = lax.axis_index("row")
    here_col = lax.axis_index("col")
    row_blocks = hess.shape[0]
    col_blocks = hess.shape[3]
    block = hess.shape[2]
    slot_count = coupling.shape[1]
    bucket = slot_count // 4
    height = row_blocks * block
    mask = pattern.astype(jnp.float32)
    grid_ids = jnp.arange(grid_rows, dtype=jnp.int32)
    dest = dest_row[0, :, 0]
    active = jnp.arange(slot_count, dtype=jnp.int32) < live[0]
    hits = (dest[:, None] == grid_ids[None, :]) & active[:, None]
    ranks = jnp.cumsum(hits.astype(jnp.int32), axis=0) - 1
    place = jnp.sum(jnp.where(hits, ranks + grid_ids[None, :] * bucket, 0), axis=1)
    place = jnp.where(active, place, grid_rows * bucket)
    outgoing = (
        jnp.zeros((grid_rows * bucket, 2, block), jnp.float32)
        .at[place]
        .set(coupling[0], mode="drop")
    )
    labels = (
        jnp.zeros((grid_rows * bucket,), jnp.float32)
        .at[place]
        .set(local_row[0].astype(jnp.float32), mode="drop")
    )
    arrived, arrived_rows = (
        lax.all_to_all(
            outgoing.reshape(grid_rows, bucket, 2, block),
            "row",
            split_axis=0,
            concat_axis=0,
            tiled=True,
        ),
        lax.all_to_all(
            labels.reshape(grid_rows, bucket), "row", split_axis=0, concat_axis=0, tiled=True
        ),
    )
    partial_value = (
        jnp.zeros((height, 2, block), jnp.float32)
        .at[arrived_rows.astype(jnp.int32).reshape(-1)]
        .add(arrived.reshape(-1, 2, block))
    )
    own = hess[:, 0, :, 0, 0, :].astype(jnp.float32).reshape(height, block)
    which = (jnp.arange(2, dtype=jnp.int32) == here_col).astype(jnp.float32)
    partial_value = partial_value + own[:, None, :] * which[None, :, None]
    corner = hess[0, 0, :, 0, 0, :].astype(jnp.float32)
    at_first = ((here_row == 0) & (here_col == 0)).astype(jnp.float32)
    at_below = ((here_row == 1) & (here_col == 0)).astype(jnp.float32)
    at_second = ((here_row == 1) & (here_col == 1)).astype(jnp.float32)
    pivots = lax.psum(
        jnp.stack([at_first * corner, at_below * corner, at_second * corner]), ("row", "col")
    )
    f00, f10, f11 = leading(pivots[0], pivots[1], pivots[2], mask[1, 0])
    mine = lax.dynamic_index_in_dim(
        mask.reshape(row_blocks, grid_rows, -1), here_row, 1, keepdims=False
    )
    rowmask = jnp.repeat(mine[:, :2], block, axis=0)
    summed = lax.psum(partial_value, "col")
    panel = panel_solve(summed * rowmask[:, :, None], f00, f10, f11)
    head_first = jnp.where(here_row == 0, f00, f10)
    head_second = jnp.where(here_row == 0, jnp.zeros_like(f11), f11)
    head = jnp.stack([head_first, head_second], 1)
    panel = panel.at[:block].set(jnp.where(here_row < 2, head, panel[:block]))
    ratio = grid_cols // grid_rows
    picked = lax.dynamic_index_in_dim(
        panel.reshape(col_blocks, ratio, block, 2, block), here_col // grid_rows, 1, keepdims=False
    )
    across = broadcast(picked, "row", here_col % grid_rows)
    left = panel.reshape(height, 2 * block)
    right = across.reshape(col_blocks * block, 2 * block)
    update = jnp.dot(left, right.T, precision=lax.Precision.HIGHEST).reshape(
        row_blocks, block, col_blocks, block
    )
    tiles = jnp.transpose(hess[:, 0, :, :, 0, :].astype(jnp.float32), (0, 2, 1, 3))
    sym = symmetric(tiles)
    block_i = jnp.arange(row_blocks, dtype=jnp.int32) * grid_rows + here_row
    block_j = jnp.arange(col_blocks, dtype=jnp.int32) * grid_cols + here_col
    links = lax.dynamic_index_in_dim(
        lax.dynamic_index_in_dim(
            mask.reshape(row_blocks, grid_rows, col_blocks, grid_cols), here_row, 1, keepdims=False
        ),
        here_col,
        2,
        keepdims=False,
    )
    same = (block_i[:, None] == block_j[None, :])[:, :, None, None]
    below = (block_i[:, None] > block_j[None, :])[:, :, None, None]
    base = jnp.where(same, sym, jnp.where(below, links[:, :, None, None] * tiles, 0.0))
    trail = base - jnp.transpose(update, (0, 2, 1, 3))
    lower_panel = jnp.transpose(panel.reshape(row_blocks, block, 2, block), (0, 2, 1, 3))
    panel_tile = lax.dynamic_index_in_dim(lower_panel, jnp.minimum(here_col, 1), 1, keepdims=False)
    in_panel = (block_j < 2)[None, :, None, None]
    kept = (block_i[:, None] >= block_j[None, :])[:, :, None, None]
    result = jnp.where(in_panel, panel_tile[:, None], jnp.where(kept, trail, 0.0))
    return jnp.transpose(result, (0, 2, 1, 3)).reshape(row_blocks, 1, block, col_blocks, 1, block)


def solution(mesh):
    return jax.shard_map(
        shards,
        mesh=mesh,
        in_specs=(
            P(None, "row", None, None, "col", None),
            P(("row", "col"), None, None, None),
            P(("row", "col"), None, None),
            P(("row", "col"), None),
            P(("row", "col")),
            P(),
        ),
        out_specs=P(None, "row", None, None, "col", None),
        check_vma=False,
    )
```

profile of v0, /device:TPU:4, one launch (start us, length us, event | category | flops | bytes accessed | tf_op | source)
XLA Modules:
  0.0 491.5 jit_solution(16189000699029080055)
XLA Ops:
  7.2 0.7 and_convert_fusion
  7.9 1.2 reduce-window.6
  9.5 0.7 convert_element_type.94
  10.2 0.8 fusion.47
  11.0 1.4 scatter_custom_fusion
  13.0 3.3 all-to-all-start
  16.3 1.0 fusion.18
  17.2 0.9 pad_maximum_fusion.3
  18.2 9.4 %copy.100 = bf16[10,1,256,5,1,256]{2,5,3,0,4,1:T(8,128)(2,1)} copy(bf16[10,1,256,5,1,256]{5,2,4,3,1,0:T(8,128)(2,1)} %param.11) | data formatting | bytes 13107200 | tf_op args[0]
  27.6 2.5 slice.121
  30.8 1.5 bitcast_convert_fusion
  32.5 4.2 broadcast_multiply_fusion.1
  37.0 0.8 copy.99
  37.8 0.9 broadcast_in_dim.117
  38.7 24.4 %scatter_fusion = f32[256,2,256]{2,1,0:T(2,128)} fusion(f32[256,2,256]{2,1,0:T(2,128)} %broadcast_in_dim.117, s32[256]{0:T(256)S(1)} %bitcast.222, f32[256,2,256]{2,1,0:T(2,128)S(1)} %bitcast.212), kind=kCustom, calls=%fused_computation.2 | custom fusion | bytes 1573888 | tf_op jit(solution)/shard_map/scatter | solution.py:73
  63.1 3.5 all-to-all-start.1
  66.7 6.9 %all-to-all-done.1 = f32[4,64,2,256]{3,2,1,0:T(2,128)S(1)} async-done(((f32[4,64,2,256]{3,2,1,0:T(2,128)}), f32[4,64,2,256]{3,2,1,0:T(2,128)S(1)}, u32[]{:S(2)}, u32[]{:S(2)}) %all-to-all-start.1) | async-done | bytes 524320 | tf_op jit(solution)/shard_map/all_to_all | solution.py:81
  73.6 29.1 %scatter_fusion.1 = f32[2560,2,256]{2,1,0:T(2,128)} fusion(f32[2560,2,256]{2,1,0:T(2,128)} %broadcast_multiply_fusion.1, s32[256]{0:T(256)S(1)} %bitcast.223, f32[256,2,256]{2,1,0:T(2,128)S(1)} %bitcast.211), kind=kCustom, calls=%fused_computation.3 | custom fusion | flops 131072 | bytes 1573888 | tf_op jit(solution)/shard_map/scatter-add | solution.py:95
  102.7 8.7 %copy.88 = f32[2560,2,256]{0,2,1:T(8,128)} copy(f32[2560,2,256]{2,1,0:T(2,128)} %scatter_fusion.1) | data formatting | bytes 10485760 | tf_op jit(solution)/shard_map/scatter-add | solution.py:95
  111.7 42.0 %all-reduce.5.cloned.1.call-done = f32[3,256,256]{2,1,0:T(8,128)} async-done(((f32[3,256,256]{2,1,0:T(8,128)}), f32[3,256,256]{2,1,0:T(8,128)}) %all-reduce.5.cloned.1.call-update) | async-done | bytes 786448 | tf_op jit(solution)/shard_map/psum | solution.py:104
  153.7 1.1 fusion.26
  155.1 1.7 fusion.29
  157.3 4.5 gather_fusion
  162.2 11.7 %cholesky.130 = f32[128,128]{1,0:T(8,128)S(1)} custom-call(f32[128,128]{1,0:T(8,128)S(1)} %cholesky.194), custom_call_target="Cholesky" | custom-call | tf_op jit(solution)/shard_map/jit(cholesky)/cholesky | solution.py:31
  174.0 9.8 %custom-call.20 = f32[1,128,128]{1,2,0:T(8,128)S(1)} custom-call(f32[1,128,128]{2,1,0:T(8,128)S(1)} %get-tuple-element.87), custom_call_target="InvertDiagBlocksLowerTriangular" | custom-call | tf_op jit(solution)/shard_map/jit(cholesky)/cholesky | solution.py:31
  184.3 11.7 %cholesky.147 = f32[128,128]{1,0:T(8,128)S(1)} custom-call(f32[128,128]{1,0:T(8,128)S(1)} %convolution_subtract_fusion.6), custom_call_target="Cholesky" | custom-call | tf_op jit(solution)/shard_map/jit(cholesky)/cholesky | solution.py:31
  198.0 3.8 while.6
  198.7 1.3 bitcast_dynamic-update-slice_fusion.4
  200.6 1.3 bitcast_dynamic-update-slice_fusion.4
  201.9 20.1 %custom-call.21 = f32[2,128,128]{1,2,0:T(8,128)S(1)} custom-call(f32[2,128,128]{2,1,0:T(8,128)S(1)} %get-tuple-element.41), custom_call_target="InvertDiagBlocksLowerTriangular" | custom-call | tf_op jit(solution)/shard_map/jit(_solve_triangular)/triangular_solve | solution.py:17
  223.7 11.7 %cholesky.164 = f32[128,128]{1,0:T(8,128)S(1)} custom-call(f32[128,128]{1,0:T(8,128)S(1)} %cholesky.197), custom_call_target="Cholesky" | custom-call | tf_op jit(solution)/shard_map/jit(cholesky)/cholesky | solution.py:34
  235.4 9.8 %custom-call.22 = f32[1,128,128]{1,2,0:T(8,128)S(1)} custom-call(f32[1,128,128]{2,1,0:T(8,128)S(1)} %get-tuple-element.83), custom_call_target="InvertDiagBlocksLowerTriangular" | custom-call | tf_op jit(solution)/shard_map/jit(cholesky)/cholesky | solution.py:34
  245.7 11.7 %cholesky.181 = f32[128,128]{1,0:T(8,128)S(1)} custom-call(f32[128,128]{1,0:T(8,128)S(1)} %convolution_subtract_fusion.5), custom_call_target="Cholesky" | custom-call | tf_op jit(solution)/shard_map/jit(cholesky)/cholesky | solution.py:34
  260.0 0.8 select_bitcast_fusion
  260.7 3.8 while.7
  261.4 1.3 bitcast_dynamic-update-slice_fusion.5
  263.3 1.3 bitcast_dynamic-update-slice_fusion.5
  264.6 20.5 %custom-call.23 = f32[2,128,128]{1,2,0:T(8,128)} custom-call(f32[2,128,128]{2,1,0:T(8,128)S(1)} %get-tuple-element.42), custom_call_target="InvertDiagBlocksLowerTriangular" | custom-call | tf_op jit(solution)/shard_map/jit(_solve_triangular)/triangular_solve | solution.py:17
  285.0 0.7 fusion.21
  285.8 54.9 %all-reduce.7.cloned.1.call-done = f32[2560,2,256]{0,2,1:T(8,128)} async-done(((f32[2560,2,256]{0,2,1:T(8,128)}), f32[2560,2,256]{0,2,1:T(8,128)}) %all-reduce.7.cloned.1.call-update) | async-done | bytes 5242896 | tf_op jit(solution)/shard_map/psum | solution.py:112
  340.7 3.0 broadcast_multiply_fusion
  343.9 2.2 copy-done.1
  346.0 1.3 fusion.13
  347.3 2.3 convolution_subtract_fusion.2
  350.0 3.5 fusion.42
  353.6 4.4 fusion.8
  358.0 1.3 fusion.11
  359.3 1.1 copy-done.2
  360.4 2.3 convolution_subtract_fusion.1
  362.7 2.8 copy.97
  365.7 1.1 copy-done.4
  366.8 2.4 fusion.34
  370.7 2.2 copy-done
  372.9 2.0 copy.107
  375.0 3.2 dot_general.16
  378.2 0.8 copy-done.9
  379.0 11.5 %convert_multiply_fusion = (f32[10,256,5,256]{1,3,2,0:T(8,128)}, f32[10,256,5,256]{1,3,2,0:T(8,128)}) fusion(bf16[10,1,256,5,1,256]{2,5,3,0,4,1:T(8,128)(2,1)} %copy.100, f32[10,5]{1,0:T(8,128)S(1)} %bitcast.215, pred[256,256]{0,1:T(8,128)(4,1)S(1)} %copy-done.9), kind=kLoop, calls=%fused_computation.8 | loop fusion | flops 9830400 | bytes 32833736 | tf_op jit(solution)/shard_map/mul | solution.py:142
  390.5 14.0 %copy.102 = f32[10,256,5,256]{3,1,2,0:T(8,128)} copy(f32[10,256,5,256]{1,3,2,0:T(8,128)} %get-tuple-element.67) | data formatting | bytes 26214400 | tf_op jit(solution)/shard_map/jit(tril)/select_n | solution.py:13
  404.5 14.1 %copy.105 = f32[10,256,5,256]{3,1,2,0:T(8,128)} copy(f32[10,256,5,256]{1,3,2,0:T(8,128)} %get-tuple-element.66) | data formatting | bytes 26214400 | tf_op jit(solution)/shard_map/mul | solution.py:142
  418.8 10.4 %copy.106 = f32[2560,2,256]{2,1,0:T(2,128)} copy(f32[2560,2,256]{2,0,1:T(8,128)} %copy-done) | data formatting | bytes 10485760 | tf_op jit(solution)/shard_map/scatter | solution.py:117
  429.2 8.0 %reshape.409 = f32[10,256,512,1]{2,1,0,3:T(8,128)} reshape(f32[2560,2,256]{2,1,0:T(2,128)} %copy.106) | data formatting | bytes 10485760 | tf_op jit(solution)/shard_map/dot_general | solution.py:125
  437.2 2.0 dynamic-slice_bitcast_fusion
  439.3 30.4 %fusion.6 = f32[10,1,256,5,1,256]{5,2,3,0,4,1:T(8,128)S(1)} fusion(f32[10,256,5,256]{3,1,2,0:T(8,128)} %copy.102, f32[10,256,5,256]{3,1,2,0:T(8,128)} %copy.105, bf16[10,1,256,5,1,256]{2,5,3,0,4,1:T(8,128)(2,1)} %copy.100, f32[10,256,256]{2,1,0:T(8,128)S(1)} %dynamic-slice_bitcast_fusion, pred[5]{0:T(512)(128)(4,1)S(1)} %broadcast_compare_fusion.3, ...), kind=kOutput, calls=%fused_computation.17 | convolution fusion | flops 20158873600 | bytes 56426652 | tf_op jit(solution)/shard_map/dot_general | solution.py:125
  469.7 15.0 %copy.108 = f32[10,1,256,5,1,256]{5,4,3,2,1,0:T(1,128)} copy(f32[10,1,256,5,1,256]{5,2,3,0,4,1:T(8,128)S(1)} %fusion.6) | data formatting | bytes 26214400 | tf_op jit(solution)/shard_map/reshape | solution.py:149
  (112 shorter events, 13.2 us)
Async XLA Ops:
  13.0 50.1 %all-to-all-start = ((f32[4,1,64]{2,1,0:T(1,128)}), f32[4,1,64]{2,1,0:T(1,128)S(1)}, u32[]{:S(2)}, u32[]{:S(2)}) async-start(f32[4,1,64]{2,1,0:T(1,128)} %all_to_all.9), calls=%async_computation | async-start | bytes 4096 | tf_op jit(solution)/shard_map/all_to_all | solution.py:88
  16.3 137.5 %all-reduce.5.cloned.1.call-start = ((), (), s32[]{:S(2)}) async-start(), calls=%async_computation.2 | async-start | bytes 1572864 | tf_op jit(solution)/shard_map/psum | solution.py:104
  27.6 2.5 copy-start.11
  32.5 6.2 %copy-start.8 = (f32[1,256,2,256]{3,2,1,0:T(2,128)S(1)}, f32[1,256,2,256]{3,2,1,0:T(2,128)}, u32[]{:S(2)}) copy-start(f32[1,256,2,256]{3,2,1,0:T(2,128)} %param.12) | copy-start | bytes 1572868
  63.1 10.5 %all-to-all-start.1 = ((f32[4,64,2,256]{3,2,1,0:T(2,128)}), f32[4,64,2,256]{3,2,1,0:T(2,128)S(1)}, u32[]{:S(2)}, u32[]{:S(2)}) async-start(f32[4,64,2,256]{3,2,1,0:T(2,128)} %bitcast.26), calls=%async_computation.1 | async-start | bytes 1048576 | tf_op jit(solution)/shard_map/all_to_all | solution.py:81
  66.5 274.1 %all-reduce.7.cloned.1.call-start = ((), (), s32[]{:S(2)}) async-start(), calls=%async_computation.3 | async-start | bytes 10485760 | tf_op jit(solution)/shard_map/psum | solution.py:112
  111.4 327.9 %all-reduce.9.cloned.1.call-start = ((), (), s32[]{:S(2)}) async-start(), calls=%async_computation.4 | async-start | bytes 5242880 | tf_op jit(solution)/shard_map/psum | solution.py:9
  153.7 3.2 copy-start.5
  343.7 2.4 copy-start.1
  353.6 4.4 copy-start.10
  359.3 1.1 copy-start.2
  365.5 1.3 copy-start.4
  366.8 2.4 copy-start.3
  369.4 1.0 copy-start.6
  369.4 1.0 copy-start.7
  370.5 2.4 copy-start
  378.2 0.8 copy-start.9
Sparse Core Ops, SparseCore 0:
  22.2 131.4 all-reduce.4
  157.4 183.2 all-reduce.6
  378.3 57.8 all-reduce.8
where the time goes:
time: 500 us; the launch traced here: 491 us
  other arithmetic  170 us (34%)
  local copies, waits for them, and re-layouts  143 us (29%)
  waiting for transfers between devices  104 us (21%)
  matrix products  50.3 us (10%)
  between operations  17 us (3%)
  starting transfers between devices  7.02 us (1%)
    psum x1, waiting for transfers between devices, shards(): summed = lax.psum(partial_value, 'col')  54.9 us
    psum x1, waiting for transfers between devices, shards(): lax.psum(jnp.stack([at_first * corner, at_below * corner, at_second * cor...  42 us
    another operation x5, other arithmetic, right_solve(): return jax.scipy.linalg.solve_triangular(lower_factor, rows.T, lower=True).T  40.6 us
    another operation x7, other arithmetic, leading(): factor11 = jnp.linalg.cholesky(reduced)  34.6 us
    another operation x6, other arithmetic, leading(): factor00 = jnp.linalg.cholesky(whole[:size, :size])  33.9 us
    dot_general x1, matrix products, shards(): jnp.dot(left, right.T, precision=lax.Precision.HIGHEST)  30.4 us
    scatter-add x1, other arithmetic, shards(): partial_value = jnp.zeros((height, 2, block), jnp.float32).at[arrived_row...  29.1 us
    scatter x1, local copies, waits for them, and re-layouts, shards(): outgoing = jnp.zeros((grid_rows * bucket, 2, block), jnp.float32).at[plac...  24.4 us
  transfers between devices with their start and end apart: 5, of which 3 were waited for; matrix products, arithmetic and copies ran while one was open for 56% of the time, Pallas kernels for 0%

commit v1 on v0

v1 whole, which is shorter than its diff:
```python
import jax
import jax.numpy as jnp
from jax import lax
from jax.sharding import PartitionSpec as P

HIGH = lax.Precision.HIGHEST


def symmetric(block):
    return jnp.tril(block) + jnp.swapaxes(jnp.tril(block, -1), -1, -2)


def lower_inverse(lower_factor):
    ident = jnp.eye(lower_factor.shape[0], dtype=lower_factor.dtype)
    return jax.scipy.linalg.solve_triangular(lower_factor, ident, lower=True)


def leading(block00, block10, block11, link):
    size = block00.shape[0]
    first = symmetric(block00)
    second = symmetric(block11)
    coupled = link * block10
    whole = jnp.concatenate(
        [jnp.concatenate([first, coupled.T], 1), jnp.concatenate([coupled, second], 1)], 0
    )
    ident = jnp.eye(2 * size, dtype=whole.dtype)
    spread = jnp.sum(jnp.abs(whole), axis=1) - jnp.abs(jnp.diagonal(whole))
    whole = whole * (1.0 - ident) + ident * (1.0 + spread)[:, None]
    factor00 = jnp.linalg.cholesky(whole[:size, :size])
    inv00 = lower_inverse(factor00)
    factor10 = jnp.dot(whole[size:, :size], inv00.T, precision=HIGH)
    reduced = whole[size:, size:] - jnp.dot(factor10, factor10.T, precision=HIGH)
    factor11 = jnp.linalg.cholesky(reduced)
    inv11 = lower_inverse(factor11)
    return factor00, factor10, factor11, inv00, inv11


def shards(hess, coupling, dest_row, local_row, live, pattern):
    grid_rows = lax.axis_size("row")
    grid_cols = lax.axis_size("col")
    here_row = lax.axis_index("row")
    here_col = lax.axis_index("col")
    row_blocks = hess.shape[0]
    col_blocks = hess.shape[3]
    block = hess.shape[2]
    slot_count = coupling.shape[1]
    bucket = slot_count // 4
    height = row_blocks * block
    width = col_blocks * block
    ratio = grid_cols // grid_rows
    mask = pattern.astype(jnp.float32)

    corner = hess[0, 0, :, 0, 0, :].astype(jnp.float32)
    at_first = ((here_row == 0) & (here_col == 0)).astype(jnp.float32)
    at_below = ((here_row == 1) & (here_col == 0)).astype(jnp.float32)
    at_second = ((here_row == 1) & (here_col == 1)).astype(jnp.float32)
    pivots = lax.psum(
        jnp.stack([at_first * corner, at_below * corner, at_second * corner]), ("row", "col")
    )

    grid_ids = jnp.arange(grid_rows, dtype=jnp.int32)
    dest = dest_row[0, :, 0]
    active = jnp.arange(slot_count, dtype=jnp.int32) < live[0]
    hits = (dest[:, None] == grid_ids[None, :]) & active[:, None]
    ranks = jnp.cumsum(hits.astype(jnp.int32), axis=0) - 1
    place = jnp.sum(jnp.where(hits, ranks + grid_ids[None, :] * bucket, 0), axis=1)
    place = jnp.where(active, place, -1)
    pick = jnp.arange(grid_rows * bucket, dtype=jnp.int32)[:, None] == place[None, :]
    outgoing = jnp.dot(
        pick.astype(jnp.float32), coupling[0].reshape(slot_count, 2 * block), precision=HIGH
    )
    labels = jnp.sum(jnp.where(pick, local_row[0][None, :], 0), axis=1).astype(jnp.float32)
    arrived = lax.all_to_all(
        outgoing.reshape(grid_rows, bucket, 2 * block), "row", split_axis=0, concat_axis=0, tiled=True
    )
    arrived_rows = lax.all_to_all(
        labels.reshape(grid_rows, bucket), "row", split_axis=0, concat_axis=0, tiled=True
    )
    spots = arrived_rows.reshape(-1).astype(jnp.int32)
    spread = jnp.arange(height, dtype=jnp.int32)[:, None] == spots[None, :]
    partial_value = jnp.dot(
        spread.astype(jnp.float32), arrived.reshape(-1, 2 * block), precision=HIGH
    ).reshape(height, 2, block)
    own = hess[:, 0, :, 0, 0, :].astype(jnp.float32).reshape(height, block)
    which = (jnp.arange(2, dtype=jnp.int32) == here_col).astype(jnp.float32)
    partial_value = partial_value + own[:, None, :] * which[None, :, None]

    f00, f10, f11, inv00, inv11 = leading(pivots[0], pivots[1], pivots[2], mask[1, 0])

    mine = lax.dynamic_index_in_dim(
        mask.reshape(row_blocks, grid_rows, -1), here_row, 1, keepdims=False
    )
    rowmask = jnp.repeat(mine[:, :2], block, axis=0)
    summed = lax.psum(partial_value, "col") * rowmask[:, :, None]
    first = jnp.dot(summed[:, 0], inv00.T, precision=HIGH)
    second = jnp.dot(
        summed[:, 1] - jnp.dot(first, f10.T, precision=HIGH), inv11.T, precision=HIGH
    )
    panel = jnp.stack([first, second], 1)
    head_first = jnp.where(here_row == 0, f00, f10)
    head_second = jnp.where(here_row == 0, jnp.zeros_like(f11), f11)
    head = jnp.stack([head_first, head_second], 1)
    panel = panel.at[:block].set(jnp.where(here_row < 2, head, panel[:block]))

    picked = lax.dynamic_index_in_dim(
        panel.reshape(col_blocks, ratio, block, 2, block), here_col // grid_rows, 1, keepdims=False
    )
    pairs = []
    for g in range(grid_rows):
        for s in range(grid_cols):
            dst_row = s % grid_rows
            dst_col = g + grid_rows * (s // grid_rows)
            pairs.append((g * grid_cols + s, dst_row * grid_cols + dst_col))
    across = lax.ppermute(picked, ("row", "col"), pairs)

    left = panel.reshape(height, 2 * block)
    right = across.reshape(width, 2 * block)
    update = jnp.dot(left, right.T, precision=HIGH)

    tiles = hess[:, 0, :, :, 0, :].astype(jnp.float32).reshape(height, width)
    block_i = jnp.arange(row_blocks, dtype=jnp.int32) * grid_rows + here_row
    block_j = jnp.arange(col_blocks, dtype=jnp.int32) * grid_cols + here_col
    links = lax.dynamic_index_in_dim(
        lax.dynamic_index_in_dim(
            mask.reshape(row_blocks, grid_rows, col_blocks, grid_cols), here_row, 1, keepdims=False
        ),
        here_col,
        2,
        keepdims=False,
    )
    full_i = jnp.repeat(block_i, block)[:, None]
    full_j = jnp.repeat(block_j, block)[None, :]
    full_links = jnp.repeat(jnp.repeat(links, block, axis=0), block, axis=1)
    result = jnp.where(full_i > full_j, full_links * tiles - update, 0.0)

    on_diag = here_row == here_col % grid_rows
    tri = jnp.arange(block)[:, None] >= jnp.arange(block)[None, :]
    for u in range(col_blocks):
        top = (u * ratio + here_col // grid_rows) * block
        own_tile = lax.dynamic_slice(tiles, (top, u * block), (block, block))
        sym_tile = jnp.where(tri, own_tile, own_tile.T)
        upd_tile = lax.dynamic_slice(update, (top, u * block), (block, block))
        old_tile = lax.dynamic_slice(result, (top, u * block), (block, block))
        new_tile = jnp.where(on_diag, sym_tile - upd_tile, old_tile)
        result = lax.dynamic_update_slice(result, new_tile, (top, u * block))

    panel_col = lax.dynamic_index_in_dim(panel, jnp.minimum(here_col, 1), 1, keepdims=False)
    result = result.at[:, :block].set(jnp.where(here_col < 2, panel_col, result[:, :block]))
    return result.reshape(row_blocks, 1, block, col_blocks, 1, block)


def solution(mesh):
    return jax.shard_map(
        shards,
        mesh=mesh,
        in_specs=(
            P(None, "row", None, None, "col", None),
            P(("row", "col"), None, None, None),
            P(("row", "col"), None, None),
            P(("row", "col"), None),
            P(("row", "col")),
            P(),
        ),
        out_specs=P(None, "row", None, None, "col", None),
        check_vma=False,
    )
```

time: 500 us -> 523 us (1.046)
  waiting for transfers between devices: 104 us -> 174 us
  local copies, waits for them, and re-layouts: 143 us -> 107 us
  other arithmetic: 170 us -> 139 us
  matrix products: 50.3 us -> 68 us
    psum x1, waiting for transfers between devices: 42 us -> 111 us  [shards(): lax.psum(jnp.stack([at_first * corner, at_below * corner, at_second * cor...]
    dot_general x3 -> x8, matrix products: 35.3 us -> 65.3 us  [the longest x1 51 us: shards(): update = jnp.dot(left, right.T, precision=HIGH)]
    scatter-add x1 -> x0, other arithmetic: 29.1 us -> none  [shards(): partial_value = jnp.zeros((height, 2, block), jnp.float32).at[arrived_row...]
    scatter x2 -> x0, local copies, waits for them, and re-layouts: 25.8 us -> none  [the longest x1 24.4 us: shards(): outgoing = jnp.zeros((grid_rows * bucket, 2, block), jnp.float32).at[plac...]
    reshape x1 -> x2, local copies, waits for them, and re-layouts: 15 us -> 32.5 us  [the longest x1 18.5 us: shards(): return result.reshape(row_blocks, 1, block, col_blocks, 1, block)]
    mul x3 -> x1, other arithmetic: 18.7 us -> 2.96 us  [shards(): summed = lax.psum(partial_value, 'col') * rowmask[:, :, None]]
    convert_element_type x1 -> x3, local copies, waits for them, and re-layouts: 0.08 us -> 14.8 us  [the longest x1 14 us: shards(): tiles = hess[:, 0, :, :, 0, :].astype(jnp.float32).reshape(height, width)]
    mul x2 -> x0, local copies, waits for them, and re-layouts: 14.3 us -> none  [shards(): links[:, :, None, None] * tiles]
  transfers between devices with their start and end apart: 5 -> 5, of which waited for: 3 -> 4; matrix products, arithmetic and copies ran while one was open for 56% -> 40% of each run, Pallas kernels for 0% -> 0%
where the time goes in v1:
time: 523 us; the launch traced here: 514 us
  waiting for transfers between devices  174 us (33%)
  other arithmetic  139 us (27%)
  local copies, waits for them, and re-layouts  107 us (20%)
  matrix products  68 us (13%)
  between operations  17.8 us (3%)
  starting transfers between devices  8.92 us (2%)
    psum x1, waiting for transfers between devices, shards(): lax.psum(jnp.stack([at_first * corner, at_below * corner, at_second * cor...  111 us
    psum x1, waiting for transfers between devices, shards(): summed = lax.psum(partial_value, 'col') * rowmask[:, :, None]  53.7 us
    dot_general x1, matrix products, shards(): update = jnp.dot(left, right.T, precision=HIGH)  51 us
    another operation x4, other arithmetic, lower_inverse(): return jax.scipy.linalg.solve_triangular(lower_factor, ident, lower=True)  40 us
    another operation x7, other arithmetic, leading(): factor11 = jnp.linalg.cholesky(reduced)  34.7 us
    another operation x6, other arithmetic, leading(): factor00 = jnp.linalg.cholesky(whole[:size, :size])  34 us
    unnamed x24, local copies, waits for them, and re-layouts  25.2 us
    reshape x1, local copies, waits for them, and re-layouts, shards(): return result.reshape(row_blocks, 1, block, col_blocks, 1, block)  18.5 us
  transfers between devices with their start and end apart: 5, of which 4 were waited for; matrix products, arithmetic and copies ran while one was open for 40% of the time, Pallas kernels for 0%

profile of v1, /device:TPU:4, one launch (start us, length us, event | category | flops | bytes accessed | tf_op | source)
XLA Modules:
  0.0 514.5 jit_solution(11993476896268605159)
XLA Ops:
  7.3 0.7 and_convert_fusion
  8.0 1.2 reduce-window.6
  9.6 0.8 fusion.61
  10.3 0.8 select_reduce_fusion
  11.1 0.7 convert_element_type.100
  11.8 3.3 all-to-all-start
  15.1 1.0 fusion.8
  16.1 0.9 pad_maximum_fusion.1
  17.1 2.5 slice.122
  20.0 1.5 bitcast_convert_fusion
  21.7 1.2 fusion.39
  22.9 3.5 all-to-all-start.1
  27.2 7.3 %all-to-all-done.1 = f32[4,64,512]{2,1,0:T(8,128)S(1)} async-done(((f32[4,64,512]{2,1,0:T(8,128)}), f32[4,64,512]{2,1,0:T(8,128)S(1)}, u32[]{:S(2)}, u32[]{:S(2)}) %all-to-all-start.1) | async-done | bytes 524320 | tf_op jit(solution)/shard_map/all_to_all | solution.py:73
  34.6 0.8 copy-done.3
  35.4 1.2 copy.81
  36.6 4.9 multiply_add_fusion
  41.6 111.1 %all-reduce.6.cloned.1.call-done = f32[3,256,256]{2,1,0:T(8,128)} async-done(((f32[3,256,256]{2,1,0:T(8,128)}), f32[3,256,256]{2,1,0:T(8,128)}) %all-reduce.6.cloned.1.call-update) | async-done | bytes 786448 | tf_op jit(solution)/shard_map/psum | solution.py:57
  152.7 1.1 fusion.35
  154.0 1.6 fusion.41
  155.7 1.2 bitcast_add_fusion.3
  157.1 4.8 gather_fusion
  162.3 11.7 %cholesky.130 = f32[128,128]{1,0:T(8,128)S(1)} custom-call(f32[128,128]{1,0:T(8,128)S(1)} %cholesky.194), custom_call_target="Cholesky" | custom-call | tf_op jit(solution)/shard_map/jit(cholesky)/cholesky | solution.py:29
  174.1 9.8 %custom-call.15 = f32[1,128,128]{1,2,0:T(8,128)S(1)} custom-call(f32[1,128,128]{2,1,0:T(8,128)S(1)} %get-tuple-element.92), custom_call_target="InvertDiagBlocksLowerTriangular" | custom-call | tf_op jit(solution)/shard_map/jit(cholesky)/cholesky | solution.py:29
  184.3 11.7 %cholesky.147 = f32[128,128]{1,0:T(8,128)S(1)} custom-call(f32[128,128]{1,0:T(8,128)S(1)} %convolution_subtract_fusion.5), custom_call_target="Cholesky" | custom-call | tf_op jit(solution)/shard_map/jit(cholesky)/cholesky | solution.py:29
  196.1 0.7 compare_reduce_fusion.2
  198.2 4.0 while.6
  198.8 1.4 bitcast_dynamic-update-slice_fusion.4
  200.8 1.4 bitcast_dynamic-update-slice_fusion.4
  202.2 20.1 %custom-call.16 = f32[2,128,128]{1,2,0:T(8,128)S(1)} custom-call(f32[2,128,128]{2,1,0:T(8,128)S(1)} %get-tuple-element.45), custom_call_target="InvertDiagBlocksLowerTriangular" | custom-call | tf_op jit(solution)/shard_map/jit(_solve_triangular)/triangular_solve | solution.py:15
  224.5 11.7 %cholesky.164 = f32[128,128]{1,0:T(8,128)S(1)} custom-call(f32[128,128]{1,0:T(8,128)S(1)} %cholesky.197), custom_call_target="Cholesky" | custom-call | tf_op jit(solution)/shard_map/jit(cholesky)/cholesky | solution.py:33
  236.3 9.8 %custom-call.17 = f32[1,128,128]{1,2,0:T(8,128)S(1)} custom-call(f32[1,128,128]{2,1,0:T(8,128)S(1)} %get-tuple-element.88), custom_call_target="InvertDiagBlocksLowerTriangular" | custom-call | tf_op jit(solution)/shard_map/jit(cholesky)/cholesky | solution.py:33
  246.6 11.7 %cholesky.181 = f32[128,128]{1,0:T(8,128)S(1)} custom-call(f32[128,128]{1,0:T(8,128)S(1)} %convolution_subtract_fusion.4), custom_call_target="Cholesky" | custom-call | tf_op jit(solution)/shard_map/jit(cholesky)/cholesky | solution.py:33
  258.3 0.7 compare_reduce_fusion.1
  259.0 0.7 compare_reduce_fusion
  261.0 4.0 while.7
  261.6 1.4 bitcast_dynamic-update-slice_fusion.5
  263.6 1.4 bitcast_dynamic-update-slice_fusion.5
  265.0 19.8 %custom-call.18 = f32[2,128,128]{1,2,0:T(8,128)S(1)} custom-call(f32[2,128,128]{2,1,0:T(8,128)S(1)} %get-tuple-element.46), custom_call_target="InvertDiagBlocksLowerTriangular" | custom-call | tf_op jit(solution)/shard_map/jit(_solve_triangular)/triangular_solve | solution.py:15
  285.8 53.7 %all-reduce.4.cloned.1.call-done = f32[2560,2,256]{2,0,1:T(8,128)} async-done(((f32[2560,2,256]{2,0,1:T(8,128)}), f32[2560,2,256]{2,0,1:T(8,128)}) %all-reduce.4.cloned.1.call-update) | async-done | bytes 5242896 | tf_op jit(solution)/shard_map/psum | solution.py:94
  339.6 3.0 broadcast_multiply_fusion
  342.5 2.4 fusion.1
  344.9 2.3 convolution_subtract_fusion
  347.3 2.4 convolution_bitcast_fusion
  350.3 2.0 copy.117
  352.5 2.1 collective-permute-start
  354.6 14.0 %copy.77 = f32[10,1,256,5,1,256]{5,3,2,0,4,1:T(8,128)} copy(bf16[10,1,256,5,1,256]{5,2,4,3,1,0:T(8,128)(2,1)} %param.13) | data formatting | bytes 19660800 | tf_op jit(solution)/shard_map/convert_element_type | solution.py:120
  368.8 15.8 %copy.110 = f32[320,8,5,256]{3,1,2,0:T(8,128)} copy(f32[320,8,5,256]{3,2,1,0:T(8,128)} %bitcast.226) | data formatting | bytes 26214400
  384.9 6.4 %broadcast_in_dim.69 = f32[2560,5,256]{0,2,1:T(8,128)} broadcast(f32[2560,5]{0,1:T(8,128)S(1)} %bitcast.237), dimensions={0,1} | broadcast | bytes 13158400 | tf_op jit(solution)/shard_map/broadcast_in_dim | solution.py:133
  391.3 14.0 %copy.78 = f32[2560,1280]{1,0:T(8,128)} copy(f32[2560,1280]{0,1:T(8,128)} %bitcast.227) | data formatting | bytes 26214400 | tf_op jit(solution)/shard_map/reshape | solution.py:133
  405.4 1.0 constant_dynamic-slice_fusion.2
  406.4 0.8 copy.104
  407.2 0.7 compare_reduce_fusion.4
  407.9 5.9 %copy.89 = f32[2560,2,256]{0,2,1:T(8,128)} copy(f32[2560,2,256]{2,0,1:T(8,128)} %copy-done) | data formatting | bytes 10485760 | tf_op jit(solution)/shard_map/scatter | solution.py:103
  413.8 1.3 collective-permute-done
  415.1 2.2 copy.113
  417.4 51.0 %subtract_select_fusion = (f32[2560,1280]{1,0:T(8,128)}, f32[2560,1280]{1,0:T(8,128)S(1)}) fusion(f32[2560,1280]{1,0:T(8,128)} %copy.78, f32[2560,1280]{1,0:T(8,128)} %bitcast.220, s32[1280]{0:T(1024)S(1)} %gt.19, s32[2560]{0:T(1024)S(1)} %gt.17, f32[2560,512]{0,1:T(8,128)S(1)} %bitcast.231, f32[1280,512]{1,0:T(8,128)S(1)} %bitcast.233), kind=kOutput, calls=%fused_computation.5 | convolution fusion | flops 20145766400 | bytes 60308480 | tf_op jit(solution)/shard_map/dot_general | solution.py:118
  468.4 4.7 copy-done.1
  473.0 2.3 constant_dynamic-slice_fusion.8
  475.9 1.9 fusion.27
  477.8 1.9 fusion.24
  479.7 1.9 fusion.21
  481.6 1.9 fusion.18
  483.5 5.1 fusion
  488.6 18.5 %reshape.290 = f32[10,1,256,5,1,256]{5,4,3,2,1,0:T(1,128)} reshape(f32[2560,1280]{1,0:T(8,128)} %fusion) | data formatting | bytes 26214400 | tf_op jit(solution)/shard_map/reshape | solution.py:149
  (105 shorter events, 11.4 us)
Async XLA Ops:
  6.5 13.0 %copy-start.5 = (s32[40,40]{1,0:T(8,128)S(1)}, s32[40,40]{1,0:T(8,128)}, u32[]{:S(2)}) copy-start(s32[40,40]{1,0:T(8,128)} %param.18) | copy-start | bytes 19204
  6.5 13.0 %copy-start.4 = (f32[1,256,2,256]{3,2,1,0:T(2,128)S(1)}, f32[1,256,2,256]{3,2,1,0:T(2,128)}, u32[]{:S(2)}) copy-start(f32[1,256,2,256]{3,2,1,0:T(2,128)} %param.14) | copy-start | bytes 1572868
  11.8 11.1 %all-to-all-start = ((f32[4,1,64]{2,1,0:T(1,128)}), f32[4,1,64]{2,1,0:T(1,128)S(1)}, u32[]{:S(2)}, u32[]{:S(2)}) async-start(f32[4,1,64]{2,1,0:T(1,128)} %convert_element_type.100), calls=%async_computation | async-start | bytes 4096 | tf_op jit(solution)/shard_map/all_to_all | solution.py:76
  15.1 137.5 %all-reduce.6.cloned.1.call-start = ((), (), s32[]{:S(2)}) async-start(), calls=%async_computation.3 | async-start | bytes 1572864 | tf_op jit(solution)/shard_map/psum | solution.py:57
  22.9 11.6 %all-to-all-start.1 = ((f32[4,64,512]{2,1,0:T(8,128)}), f32[4,64,512]{2,1,0:T(8,128)S(1)}, u32[]{:S(2)}, u32[]{:S(2)}) async-start(f32[4,64,512]{2,1,0:T(8,128)} %fusion.39), calls=%async_computation.1 | async-start | bytes 1048576 | tf_op jit(solution)/shard_map/all_to_all | solution.py:73
  26.4 313.1 %all-reduce.4.cloned.1.call-start = ((), (), s32[]{:S(2)}) async-start(), calls=%async_computation.2 | async-start | bytes 10485760 | tf_op jit(solution)/shard_map/psum | solution.py:94
  34.6 0.8 copy-start.3
  350.1 2.4 copy-start
  352.5 62.6 %collective-permute-start = (f32[5,256,2,256]{3,2,1,0:T(2,128)S(1)}, f32[5,256,2,256]{3,2,1,0:T(2,128)}, u32[]{:S(2)}, u32[]{:S(2)}) collective-permute-start(f32[5,256,2,256]{3,2,1,0:T(2,128)S(1)} %bitcast.234), channel_id=1, source_target_pairs={{0,0},{1,8},{2,16},{3,24},{4,4},{5,12},{6,20},{7,28},{8,1},{9,9},{... | collective-permute-start | bytes 7864328 | tf_op jit(solution)/shard_map/ppermute | solution.py:114
  413.8 3.5 copy-start.2
  468.4 4.7 copy-start.1
Sparse Core Ops, SparseCore 0:
  21.1 131.5 all-reduce.5
  156.4 183.1 all-reduce.3

commit v2 on v1

--- a/solution.py
+++ b/solution.py
@@ -51,12 +51,20 @@
     mask = pattern.astype(jnp.float32)
 
     corner = hess[0, 0, :, 0, 0, :].astype(jnp.float32)
-    at_first = ((here_row == 0) & (here_col == 0)).astype(jnp.float32)
-    at_below = ((here_row == 1) & (here_col == 0)).astype(jnp.float32)
-    at_second = ((here_row == 1) & (here_col == 1)).astype(jnp.float32)
-    pivots = lax.psum(
-        jnp.stack([at_first * corner, at_below * corner, at_second * corner]), ("row", "col")
-    )
+    devices = grid_rows * grid_cols
+    here = here_row * grid_cols + here_col
+    pivots = []
+    for source in (0, grid_cols, grid_cols + 1):
+        value = jnp.where(here == source, corner, 0.0)
+        reach = 1
+        while reach < devices:
+            pairs = [
+                ((source + m) % devices, (source + m + reach) % devices)
+                for m in range(min(reach, devices - reach))
+            ]
+            value = value + lax.ppermute(value, ("row", "col"), pairs)
+            reach *= 2
+        pivots.append(value)
 
     grid_ids = jnp.arange(grid_rows, dtype=jnp.int32)
     dest = dest_row[0, :, 0]
@@ -91,12 +99,24 @@
         mask.reshape(row_blocks, grid_rows, -1), here_row, 1, keepdims=False
     )
     rowmask = jnp.repeat(mine[:, :2], block, axis=0)
-    summed = lax.psum(partial_value, "col") * rowmask[:, :, None]
+    chunk = height // grid_cols
+    pieces = lax.all_to_all(
+        partial_value.reshape(grid_cols, chunk, 2, block), "col", split_axis=0, concat_axis=0, tiled=True
+    )
+    chunk_mask = lax.dynamic_slice_in_dim(rowmask, here_col * chunk, chunk, 0)
+    summed = jnp.sum(pieces, axis=0) * chunk_mask[:, :, None]
     first = jnp.dot(summed[:, 0], inv00.T, precision=HIGH)
     second = jnp.dot(
         summed[:, 1] - jnp.dot(first, f10.T, precision=HIGH), inv11.T, precision=HIGH
     )
-    panel = jnp.stack([first, second], 1)
+    solved = jnp.stack([first, second], 1)
+    panel = lax.all_to_all(
+        jnp.broadcast_to(solved[None], (grid_cols, chunk, 2, block)),
+        "col",
+        split_axis=0,
+        concat_axis=0,
+        tiled=True,
+    ).reshape(height, 2, block)
     head_first = jnp.where(here_row == 0, f00, f10)
     head_second = jnp.where(here_row == 0, jnp.zeros_like(f11), f11)
     head = jnp.stack([head_first, head_second], 1)
@@ -115,7 +135,7 @@
 
     left = panel.reshape(height, 2 * block)
     right = across.reshape(width, 2 * block)
-    update = jnp.dot(left, right.T, precision=HIGH)
+    update = jnp.dot(left, right.T, precision=lax.Precision.HIGH)
 
     tiles = hess[:, 0, :, :, 0, :].astype(jnp.float32).reshape(height, width)
     block_i = jnp.arange(row_blocks, dtype=jnp.int32) * grid_rows + here_row

time: 523 us -> 597 us (1.14)
  waiting for transfers between devices: 174 us -> 254 us
  starting transfers between devices: 8.92 us -> 39.9 us
  matrix products: 68 us -> 39.5 us
  between operations: 17.8 us -> 4.44 us
  local copies, waits for them, and re-layouts: 107 us -> 113 us
    psum x2 -> x0, waiting for transfers between devices: 165 us -> none  [the longest x1 111 us: shards(): lax.psum(jnp.stack([at_first * corner, at_below * corner, at_second * cor...]
    ppermute x0 -> x15, waiting for transfers between devices: none -> 130 us  [shards(): value = value + lax.ppermute(value, ('row', 'col'), pairs)]
    all_to_all x0 -> x2, waiting for transfers between devices: none -> 116 us  [the longest x1 116 us: shards(): lax.all_to_all(jnp.broadcast_to(solved[None], (grid_cols, chunk, 2, block...]
    dot_general x1, matrix products: 51 us -> 30.7 us  [shards(): update = jnp.dot(left, right.T, precision=lax.Precision.HIGH)]
    ppermute x0 -> x15, starting transfers between devices: none -> 18.7 us  [shards(): value = value + lax.ppermute(value, ('row', 'col'), pairs)]
    all_to_all x0 -> x2, starting transfers between devices: none -> 9.29 us  [the longest x1 4.64 us: shards(): lax.all_to_all(partial_value.reshape(grid_cols, chunk, 2, block), 'col',...]
    unnamed x24 -> x18, local copies, waits for them, and re-layouts: 25.2 us -> 22 us
  transfers between devices with their start and end apart: 5 -> 20, of which waited for: 4 -> 8; matrix products, arithmetic and copies ran while one was open for 40% -> 35% of each run, Pallas kernels for 0% -> 0%
where the time goes in v2:
time: 597 us; the launch traced here: 589 us
  waiting for transfers between devices  254 us (43%)
  other arithmetic  137 us (23%)
  local copies, waits for them, and re-layouts  113 us (19%)
  starting transfers between devices  39.9 us (7%)
  matrix products  39.5 us (7%)
    ppermute x15, waiting for transfers between devices, shards(): value = value + lax.ppermute(value, ('row', 'col'), pairs)  130 us
    all_to_all x1, waiting for transfers between devices, shards(): lax.all_to_all(jnp.broadcast_to(solved[None], (grid_cols, chunk, 2, block...  116 us
    another operation x4, other arithmetic, lower_inverse(): return jax.scipy.linalg.solve_triangular(lower_factor, ident, lower=True)  40 us
    another operation x7, other arithmetic, leading(): factor11 = jnp.linalg.cholesky(reduced)  34.7 us
    another operation x6, other arithmetic, leading(): factor00 = jnp.linalg.cholesky(whole[:size, :size])  34 us
    dot_general x1, matrix products, shards(): update = jnp.dot(left, right.T, precision=lax.Precision.HIGH)  30.7 us
    unnamed x18, local copies, waits for them, and re-layouts  22 us
    ppermute x15, starting transfers between devices, shards(): value = value + lax.ppermute(value, ('row', 'col'), pairs)  18.7 us
  transfers between devices with their start and end apart: 20, of which 8 were waited for; matrix products, arithmetic and copies ran while one was open for 35% of the time, Pallas kernels for 0%

profile of v2, /device:TPU:4, one launch (start us, length us, event | category | flops | bytes accessed | tf_op | source)
XLA Modules:
  0.0 588.8 jit_solution(1819591221686720474)
XLA Ops:
  1.4 1.2 reduce-window.6
  5.2 3.3 all-to-all-start
  8.5 1.8 fusion.6
  11.0 1.4 collective-permute-start.5
  12.4 1.4 collective-permute-start.10
  13.7 1.5 reshape.274
  15.2 1.2 fusion.37
  16.4 2.5 slice.113
  18.9 6.7 %all-to-all-start.1 = ((f32[4,64,512]{2,1,0:T(8,128)}), f32[4,64,512]{2,1,0:T(8,128)S(1)}, u32[]{:S(2)}, u32[]{:S(2)}) async-start(f32[4,64,512]{2,1,0:T(8,128)} %fusion.37), calls=%async_computation.1 | async-start | bytes 1048576 | tf_op jit(solution)/shard_map/all_to_all | solution.py:81
  25.6 1.5 bitcast_convert_fusion
  27.2 5.5 all-to-all-done.1
  33.5 1.2 copy.140
  34.8 2.5 multiply_add_fusion
  37.3 2.7 copy.141
  40.0 4.6 all-to-all-start.2
  44.7 1.2 fusion.57
  48.9 1.3 collective-permute-start.12
  51.8 124.0 %collective-permute-done.12 = f32[256,256]{1,0:T(8,128)S(1)} collective-permute-done((f32[256,256]{1,0:T(8,128)S(1)}, f32[256,256]{1,0:T(8,128)S(1)}, u32[]{:S(2)}, u32[]{:S(2)}) %collective-permute-start.12) | collective-permute-done | bytes 262176 | tf_op jit(solution)/shard_map/ppermute | solution.py:65
  175.8 1.3 collective-permute-start.13
  177.2 1.3 collective-permute-start.8
  178.6 1.3 collective-permute-start.4
  180.0 4.6 collective-permute-start.14
  185.8 1.5 collective-permute-start.9
  187.3 2.3 collective-permute-done.4
  190.5 2.6 collective-permute-done.9
  194.4 4.5 gather_fusion
  199.4 11.7 %cholesky.130 = f32[128,128]{1,0:T(8,128)S(1)} custom-call(f32[128,128]{1,0:T(8,128)S(1)} %cholesky.194), custom_call_target="Cholesky" | custom-call | tf_op jit(solution)/shard_map/jit(cholesky)/cholesky | solution.py:29
  211.1 9.8 %custom-call.15 = f32[1,128,128]{1,2,0:T(8,128)S(1)} custom-call(f32[1,128,128]{2,1,0:T(8,128)S(1)} %get-tuple-element.89), custom_call_target="InvertDiagBlocksLowerTriangular" | custom-call | tf_op jit(solution)/shard_map/jit(cholesky)/cholesky | solution.py:29
  221.4 11.7 %cholesky.147 = f32[128,128]{1,0:T(8,128)S(1)} custom-call(f32[128,128]{1,0:T(8,128)S(1)} %convolution_subtract_fusion.5), custom_call_target="Cholesky" | custom-call | tf_op jit(solution)/shard_map/jit(cholesky)/cholesky | solution.py:29
  235.3 4.1 while.6
  236.0 1.3 bitcast_dynamic-update-slice_fusion.4
  238.0 1.3 bitcast_dynamic-update-slice_fusion.4
  239.4 20.1 %custom-call.16 = f32[2,128,128]{1,2,0:T(8,128)S(1)} custom-call(f32[2,128,128]{2,1,0:T(8,128)S(1)} %get-tuple-element.45), custom_call_target="InvertDiagBlocksLowerTriangular" | custom-call | tf_op jit(solution)/shard_map/jit(_solve_triangular)/triangular_solve | solution.py:15
  261.6 11.7 %cholesky.164 = f32[128,128]{1,0:T(8,128)S(1)} custom-call(f32[128,128]{1,0:T(8,128)S(1)} %cholesky.197), custom_call_target="Cholesky" | custom-call | tf_op jit(solution)/shard_map/jit(cholesky)/cholesky | solution.py:33
  273.4 9.8 %custom-call.17 = f32[1,128,128]{1,2,0:T(8,128)S(1)} custom-call(f32[1,128,128]{2,1,0:T(8,128)S(1)} %get-tuple-element.85), custom_call_target="InvertDiagBlocksLowerTriangular" | custom-call | tf_op jit(solution)/shard_map/jit(cholesky)/cholesky | solution.py:33
  283.7 11.7 %cholesky.181 = f32[128,128]{1,0:T(8,128)S(1)} custom-call(f32[128,128]{1,0:T(8,128)S(1)} %convolution_subtract_fusion.4), custom_call_target="Cholesky" | custom-call | tf_op jit(solution)/shard_map/jit(cholesky)/cholesky | solution.py:33
  298.2 4.2 while.7
  298.9 1.4 bitcast_dynamic-update-slice_fusion.5
  301.0 1.4 bitcast_dynamic-update-slice_fusion.5
  302.4 19.8 %custom-call.18 = f32[2,128,128]{1,2,0:T(8,128)S(1)} custom-call(f32[2,128,128]{2,1,0:T(8,128)S(1)} %get-tuple-element.46), custom_call_target="InvertDiagBlocksLowerTriangular" | custom-call | tf_op jit(solution)/shard_map/jit(_solve_triangular)/triangular_solve | solution.py:15
  323.2 2.9 reduce_sum.38
  327.7 2.9 broadcast_in_dim.91
  330.6 4.6 all-to-all-start.3
  335.3 116.4 %all-to-all-done.3 = f32[8,320,2,256]{3,1,2,0:T(8,128)} async-done(((f32[8,320,2,256]{3,1,2,0:T(8,128)}), f32[8,320,2,256]{3,1,2,0:T(8,128)}, u32[]{:S(2)}, u32[]{:S(2)}) %all-to-all-start.3) | async-done | bytes 5242912 | tf_op jit(solution)/shard_map/all_to_all | solution.py:113
  451.7 2.8 copy.150
  454.7 2.4 copy-done
  457.3 2.0 copy.180
  459.3 1.9 collective-permute-start.15
  461.2 14.0 %copy.136 = f32[10,1,256,5,1,256]{5,3,2,0,4,1:T(8,128)} copy(bf16[10,1,256,5,1,256]{5,2,4,3,1,0:T(8,128)(2,1)} %param.13) | data formatting | bytes 19660800 | tf_op jit(solution)/shard_map/convert_element_type | solution.py:140
  475.4 16.0 %copy.173 = f32[320,8,5,256]{3,1,2,0:T(8,128)} copy(f32[320,8,5,256]{3,2,1,0:T(8,128)} %bitcast.211) | data formatting | bytes 26214400
  491.7 6.4 %broadcast_in_dim.82 = f32[2560,5,256]{0,2,1:T(8,128)} broadcast(f32[2560,5]{0,1:T(8,128)S(1)} %bitcast.232), dimensions={0,1} | broadcast | bytes 13158400 | tf_op jit(solution)/shard_map/broadcast_in_dim | solution.py:153
  498.1 14.0 %copy.137 = f32[2560,1280]{1,0:T(8,128)} copy(f32[2560,1280]{0,1:T(8,128)} %bitcast.219) | data formatting | bytes 26214400 | tf_op jit(solution)/shard_map/reshape | solution.py:153
  512.2 1.0 constant_dynamic-slice_fusion.2
  514.1 5.9 copy.151
  519.9 2.0 collective-permute-done.15
  521.9 2.0 copy.176
  523.9 30.7 %subtract_select_fusion = (f32[2560,1280]{1,0:T(8,128)}, f32[2560,1280]{1,0:T(8,128)}) fusion(f32[2560,1280]{1,0:T(8,128)} %copy.137, f32[2560,1280]{1,0:T(8,128)} %bitcast.213, s32[1280]{0:T(1024)S(1)} %gt.19, s32[2560]{0:T(1024)S(1)} %gt.17, f32[2560,512]{0,1:T(8,128)} %bitcast.224, f32[1280,512]{1,0:T(8,128)S(1)} %bitcast.225), kind=kOutput, calls=%fused_computation.5 | convolution fusion | flops 10079436800 | bytes 60308480 | tf_op jit(solution)/shard_map/dot_general | solution.py:138
  554.6 2.3 constant_dynamic-slice_fusion.9
  557.5 1.9 fusion.25
  559.4 1.9 fusion.22
  561.3 1.9 fusion.19
  563.2 1.9 fusion.16
  565.0 5.1 fusion
  570.1 18.5 %reshape.277 = f32[10,1,256,5,1,256]{5,4,3,2,1,0:T(1,128)} reshape(f32[2560,1280]{1,0:T(8,128)} %fusion) | data formatting | bytes 26214400 | tf_op jit(solution)/shard_map/reshape | solution.py:169
  (142 shorter events, 26.1 us)
Async XLA Ops:
  5.2 13.7 %all-to-all-start = ((f32[4,1,64]{2,1,0:T(1,128)}), f32[4,1,64]{2,1,0:T(1,128)S(1)}, u32[]{:S(2)}, u32[]{:S(2)}) async-start(f32[4,1,64]{2,1,0:T(1,128)} %convert_element_type.76), calls=%async_computation | async-start | bytes 4096 | tf_op jit(solution)/shard_map/all_to_all | solution.py:84
  10.3 34.4 %collective-permute-start = (f32[256,256]{1,0:T(8,128)}, f32[256,256]{1,0:T(8,128)S(1)}, u32[]{:S(2)}, u32[]{:S(2)}) collective-permute-start(f32[256,256]{1,0:T(8,128)} %get-tuple-element.75), channel_id=1, source_target_pairs={{0,1}} | collective-permute-start | bytes 786440 | tf_op jit(solution)/shard_map/ppermute | solution.py:65
  11.0 33.7 %collective-permute-start.5 = (f32[256,256]{1,0:T(8,128)}, f32[256,256]{1,0:T(8,128)}, u32[]{:S(2)}, u32[]{:S(2)}) collective-permute-start(f32[256,256]{1,0:T(8,128)} %get-tuple-element.77), channel_id=1, source_target_pairs={{8,9}} | collective-permute-start | bytes 786440 | tf_op jit(solution)/shard_map/ppermute | solution.py:65
  12.4 32.3 %collective-permute-start.10 = (f32[256,256]{1,0:T(8,128)}, f32[256,256]{1,0:T(8,128)}, u32[]{:S(2)}, u32[]{:S(2)}) collective-permute-start(f32[256,256]{1,0:T(8,128)} %get-tuple-element.76), channel_id=1, source_target_pairs={{9,10}} | collective-permute-start | bytes 786440 | tf_op jit(solution)/shard_map/ppermute | solution.py:65
  18.9 13.8 %all-to-all-start.1 = ((f32[4,64,512]{2,1,0:T(8,128)}), f32[4,64,512]{2,1,0:T(8,128)S(1)}, u32[]{:S(2)}, u32[]{:S(2)}) async-start(f32[4,64,512]{2,1,0:T(8,128)} %fusion.37), calls=%async_computation.1 | async-start | bytes 1048576 | tf_op jit(solution)/shard_map/all_to_all | solution.py:81
  32.7 0.8 copy-start.1
  37.3 11.4 %copy-start.2 = (s32[40,40]{1,0:T(8,128)S(1)}, s32[40,40]{1,0:T(8,128)}, u32[]{:S(2)}) copy-start(s32[40,40]{1,0:T(8,128)} %param.18) | copy-start | bytes 19204
  40.0 283.1 %all-to-all-start.2 = ((f32[8,320,2,256]{3,1,2,0:T(8,128)}), f32[8,320,2,256]{3,1,2,0:T(8,128)}, u32[]{:S(2)}, u32[]{:S(2)}) async-start(f32[8,320,2,256]{3,1,2,0:T(8,128)} %copy.141), calls=%async_computation.2 | async-start | bytes 10485760 | tf_op jit(solution)/shard_map/all_to_all | solution.py:103
  45.9 2.1 collective-permute-start.1
  46.6 2.3 collective-permute-start.11
  47.3 2.9 collective-permute-start.6
  48.0 2.9 collective-permute-start.2
  48.9 126.9 %collective-permute-start.12 = (f32[256,256]{1,0:T(8,128)S(1)}, f32[256,256]{1,0:T(8,128)S(1)}, u32[]{:S(2)}, u32[]{:S(2)}) collective-permute-start(f32[256,256]{1,0:T(8,128)S(1)} %add.230), channel_id=1, source_target_pairs={{9,13},{10,14},{11,15},{12,16}} | collective-permute-start | bytes 786440 | tf_op jit(solution)/shard_map/ppermute | solution.py:65
  50.2 126.9 %collective-permute-start.7 = (f32[256,256]{1,0:T(8,128)S(1)}, f32[256,256]{1,0:T(8,128)S(1)}, u32[]{:S(2)}, u32[]{:S(2)}) collective-permute-start(f32[256,256]{1,0:T(8,128)S(1)} %add.225), channel_id=1, source_target_pairs={{8,12},{9,13},{10,14},{11,15}} | collective-permute-start | bytes 786440 | tf_op jit(solution)/shard_map/ppermute | solution.py:65
  51.0 127.6 %collective-permute-start.3 = (f32[256,256]{1,0:T(8,128)S(1)}, f32[256,256]{1,0:T(8,128)S(1)}, u32[]{:S(2)}, u32[]{:S(2)}) collective-permute-start(f32[256,256]{1,0:T(8,128)S(1)} %add.219), channel_id=1, source_target_pairs={{0,8},{1,9},{2,10},{3,11},{4,12},{5,13},{6,14},{7,15}} | collective-permute-start | bytes 786440 | tf_op jit(solution)/shard_map/ppermute | solution.py:65
  175.8 4.1 collective-permute-start.13
  177.2 8.6 %collective-permute-start.8 = (f32[256,256]{1,0:T(8,128)S(1)}, f32[256,256]{1,0:T(8,128)S(1)}, u32[]{:S(2)}, u32[]{:S(2)}) collective-permute-start(f32[256,256]{1,0:T(8,128)S(1)} %add.226), channel_id=1, source_target_pairs={{8,16},{9,17},{10,18},{11,19},{12,20},{13,21},{14,22},{15,23}} | collective-permute-start | bytes 786440 | tf_op jit(solution)/shard_map/ppermute | solution.py:65
  178.6 11.1 %collective-permute-start.4 = (f32[256,256]{1,0:T(8,128)S(1)}, f32[256,256]{1,0:T(8,128)S(1)}, u32[]{:S(2)}, u32[]{:S(2)}) collective-permute-start(f32[256,256]{1,0:T(8,128)S(1)} %add.220), channel_id=1, source_target_pairs={{0,16},{1,17},{2,18},{3,19},{4,20},{5,21},{6,22},{7,23},{8,24},{9,... | collective-permute-start | bytes 786440 | tf_op jit(solution)/shard_map/ppermute | solution.py:65
  180.0 10.4 %collective-permute-start.14 = (f32[256,256]{1,0:T(8,128)S(1)}, f32[256,256]{1,0:T(8,128)S(1)}, u32[]{:S(2)}, u32[]{:S(2)}) collective-permute-start(f32[256,256]{1,0:T(8,128)S(1)} %add.232), channel_id=1, source_target_pairs={{9,25},{10,26},{11,27},{12,28},{13,29},{14,30},{15,31},{16,0},{17,... | collective-permute-start | bytes 786440 | tf_op jit(solution)/shard_map/ppermute | solution.py:65
  185.8 7.4 %collective-permute-start.9 = (f32[256,256]{1,0:T(8,128)S(1)}, f32[256,256]{1,0:T(8,128)S(1)}, u32[]{:S(2)}, u32[]{:S(2)}) collective-permute-start(f32[256,256]{1,0:T(8,128)S(1)} %add.227), channel_id=1, source_target_pairs={{8,24},{9,25},{10,26},{11,27},{12,28},{13,29},{14,30},{15,31},{16,... | collective-permute-start | bytes 786440 | tf_op jit(solution)/shard_map/ppermute | solution.py:65
  330.6 121.1 %all-to-all-start.3 = ((f32[8,320,2,256]{3,1,2,0:T(8,128)}), f32[8,320,2,256]{3,1,2,0:T(8,128)}, u32[]{:S(2)}, u32[]{:S(2)}) async-start(f32[8,320,2,256]{3,1,2,0:T(8,128)} %broadcast_in_dim.91), calls=%async_computation.3 | async-start | bytes 10485760 | tf_op jit(solution)/shard_map/all_to_all | solution.py:113
  454.7 2.4 copy-start
  459.3 62.6 %collective-permute-start.15 = (f32[5,256,2,256]{3,2,1,0:T(2,128)S(1)}, f32[5,256,2,256]{3,2,1,0:T(2,128)}, u32[]{:S(2)}, u32[]{:S(2)}) collective-permute-start(f32[5,256,2,256]{3,2,1,0:T(2,128)S(1)} %bitcast.229), channel_id=1, source_target_pairs={{0,0},{1,8},{2,16},{3,24},{4,4},{5,12},{6,20},{7,28},{8,1},{9,9},{... | collective-permute-start | bytes 7864328 | tf_op jit(solution)/shard_map/ppermute | solution.py:134

commit v3 on v2

--- a/solution.py
+++ b/solution.py
@@ -93,34 +93,61 @@
     which = (jnp.arange(2, dtype=jnp.int32) == here_col).astype(jnp.float32)
     partial_value = partial_value + own[:, None, :] * which[None, :, None]
 
-    f00, f10, f11, inv00, inv11 = leading(pivots[0], pivots[1], pivots[2], mask[1, 0])
-
     mine = lax.dynamic_index_in_dim(
         mask.reshape(row_blocks, grid_rows, -1), here_row, 1, keepdims=False
     )
     rowmask = jnp.repeat(mine[:, :2], block, axis=0)
     chunk = height // grid_cols
+    partial_value, pivots = lax.optimization_barrier((partial_value, pivots))
     pieces = lax.all_to_all(
         partial_value.reshape(grid_cols, chunk, 2, block), "col", split_axis=0, concat_axis=0, tiled=True
     )
     chunk_mask = lax.dynamic_slice_in_dim(rowmask, here_col * chunk, chunk, 0)
     summed = jnp.sum(pieces, axis=0) * chunk_mask[:, :, None]
-    first = jnp.dot(summed[:, 0], inv00.T, precision=HIGH)
-    second = jnp.dot(
-        summed[:, 1] - jnp.dot(first, f10.T, precision=HIGH), inv11.T, precision=HIGH
-    )
-    solved = jnp.stack([first, second], 1)
-    panel = lax.all_to_all(
-        jnp.broadcast_to(solved[None], (grid_cols, chunk, 2, block)),
+    assembled = lax.all_to_all(
+        jnp.broadcast_to(summed[None], (grid_cols, chunk, 2, block)),
         "col",
         split_axis=0,
         concat_axis=0,
         tiled=True,
     ).reshape(height, 2, block)
+    tiles = hess[:, 0, :, :, 0, :].astype(jnp.float32).reshape(height, width)
+    block_i = jnp.arange(row_blocks, dtype=jnp.int32) * grid_rows + here_row
+    block_j = jnp.arange(col_blocks, dtype=jnp.int32) * grid_cols + here_col
+    links = lax.dynamic_index_in_dim(
+        lax.dynamic_index_in_dim(
+            mask.reshape(row_blocks, grid_rows, col_blocks, grid_cols), here_row, 1, keepdims=False
+        ),
+        here_col,
+        2,
+        keepdims=False,
+    )
+    full_i = jnp.repeat(block_i, block)[:, None]
+    full_j = jnp.repeat(block_j, block)[None, :]
+    full_links = jnp.repeat(jnp.repeat(links, block, axis=0), block, axis=1)
+    base = jnp.where(full_i > full_j, full_links * tiles, 0.0)
+    on_diag = here_row == here_col % grid_rows
+    tri = jnp.arange(block)[:, None] >= jnp.arange(block)[None, :]
+    for u in range(col_blocks):
+        top = (u * ratio + here_col // grid_rows) * block
+        own_tile = lax.dynamic_slice(tiles, (top, u * block), (block, block))
+        sym_tile = jnp.where(tri, own_tile, own_tile.T)
+        old_tile = lax.dynamic_slice(base, (top, u * block), (block, block))
+        base = lax.dynamic_update_slice(
+            base, jnp.where(on_diag, sym_tile, old_tile), (top, u * block)
+        )
+    base, assembled = lax.optimization_barrier((base, assembled))
+    f00, f10, f11, inv00, inv11 = leading(pivots[0], pivots[1], pivots[2], mask[1, 0])
+    first = jnp.dot(assembled[:, 0], inv00.T, precision=HIGH)
+    second = jnp.dot(
+        assembled[:, 1] - jnp.dot(first, f10.T, precision=HIGH), inv11.T, precision=HIGH
+    )
+    panel = jnp.stack([first, second], 1)
     head_first = jnp.where(here_row == 0, f00, f10)
     head_second = jnp.where(here_row == 0, jnp.zeros_like(f11), f11)
     head = jnp.stack([head_first, head_second], 1)
     panel = panel.at[:block].set(jnp.where(here_row < 2, head, panel[:block]))
+
 
     picked = lax.dynamic_index_in_dim(
         panel.reshape(col_blocks, ratio, block, 2, block), here_col // grid_rows, 1, keepdims=False
@@ -136,34 +163,7 @@
     left = panel.reshape(height, 2 * block)
     right = across.reshape(width, 2 * block)
     update = jnp.dot(left, right.T, precision=lax.Precision.HIGH)
-
-    tiles = hess[:, 0, :, :, 0, :].astype(jnp.float32).reshape(height, width)
-    block_i = jnp.arange(row_blocks, dtype=jnp.int32) * grid_rows + here_row
-    block_j = jnp.arange(col_blocks, dtype=jnp.int32) * grid_cols + here_col
-    links = lax.dynamic_index_in_dim(
-        lax.dynamic_index_in_dim(
-            mask.reshape(row_blocks, grid_rows, col_blocks, grid_cols), here_row, 1, keepdims=False
-        ),
-        here_col,
-        2,
-        keepdims=False,
-    )
-    full_i = jnp.repeat(block_i, block)[:, None]
-    full_j = jnp.repeat(block_j, block)[None, :]
-    full_links = jnp.repeat(jnp.repeat(links, block, axis=0), block, axis=1)
-    result = jnp.where(full_i > full_j, full_links * tiles - update, 0.0)
-
-    on_diag = here_row == here_col % grid_rows
-    tri = jnp.arange(block)[:, None] >= jnp.arange(block)[None, :]
-    for u in range(col_blocks):
-        top = (u * ratio + here_col // grid_rows) * block
-        own_tile = lax.dynamic_slice(tiles, (top, u * block), (block, block))
-        sym_tile = jnp.where(tri, own_tile, own_tile.T)
-        upd_tile = lax.dynamic_slice(update, (top, u * block), (block, block))
-        old_tile = lax.dynamic_slice(result, (top, u * block), (block, block))
-        new_tile = jnp.where(on_diag, sym_tile - upd_tile, old_tile)
-        result = lax.dynamic_update_slice(result, new_tile, (top, u * block))
-
+    result = base - jnp.where(full_i >= full_j, update, 0.0)
     panel_col = lax.dynamic_index_in_dim(panel, jnp.minimum(here_col, 1), 1, keepdims=False)
     result = result.at[:, :block].set(jnp.where(here_col < 2, panel_col, result[:, :block]))
     return result.reshape(row_blocks, 1, block, col_blocks, 1, block)

time: 597 us -> 480 us (0.80)
  waiting for transfers between devices: 254 us -> 109 us
  other arithmetic: 137 us -> 156 us
  starting transfers between devices: 39.9 us -> 50.4 us
    ppermute x15, waiting for transfers between devices: 130 us -> 5.09 us  [shards(): value = value + lax.ppermute(value, ('row', 'col'), pairs)]
    all_to_all x1, waiting for transfers between devices: 116 us -> 0.01 us  [shards(): lax.all_to_all(jnp.broadcast_to(summed[None], (grid_cols, chunk, 2, block...]
    ppermute x1, waiting for transfers between devices: 2.01 us -> 51.2 us  [shards(): across = lax.ppermute(picked, ('row', 'col'), pairs)]
    all_to_all x1, waiting for transfers between devices: 0.01 us -> 47.2 us  [shards(): lax.all_to_all(partial_value.reshape(grid_cols, chunk, 2, block), 'col',...]
    select_n x0 -> x1, other arithmetic: none -> 14.6 us  [shards(): base = jnp.where(full_i > full_j, full_links * tiles, 0.0)]
    unnamed x18 -> x26, local copies, waits for them, and re-layouts: 22 us -> 19.7 us
    another operation x6 -> x7, other arithmetic: 34 us -> 34.6 us  [leading(): factor00 = jnp.linalg.cholesky(whole[:size, :size])]
  transfers between devices with their start and end apart: 20 -> 20, of which waited for: 8 -> 6; matrix products, arithmetic and copies ran while one was open for 35% -> 49% of each run, Pallas kernels for 0% -> 0%
where the time goes in v3:
time: 480 us; the launch traced here: 472 us
  other arithmetic  156 us (32%)
  local copies, waits for them, and re-layouts  110 us (23%)
  waiting for transfers between devices  109 us (23%)
  starting transfers between devices  50.4 us (10%)
  matrix products  41.6 us (9%)
    ppermute x1, waiting for transfers between devices, shards(): across = lax.ppermute(picked, ('row', 'col'), pairs)  51.2 us
    all_to_all x1, waiting for transfers between devices, shards(): lax.all_to_all(partial_value.reshape(grid_cols, chunk, 2, block), 'col',...  47.2 us
    another operation x4, other arithmetic, lower_inverse(): return jax.scipy.linalg.solve_triangular(lower_factor, ident, lower=True)  39.8 us
    another operation x7, other arithmetic, leading(): factor11 = jnp.linalg.cholesky(reduced)  34.6 us
    another operation x7, other arithmetic, leading(): factor00 = jnp.linalg.cholesky(whole[:size, :size])  34.6 us
    dot_general x1, matrix products, shards(): update = jnp.dot(left, right.T, precision=lax.Precision.HIGH)  27 us
    unnamed x26, local copies, waits for them, and re-layouts  19.7 us
    ppermute x15, starting transfers between devices, shards(): value = value + lax.ppermute(value, ('row', 'col'), pairs)  18.5 us
  transfers between devices with their start and end apart: 20, of which 6 were waited for; matrix products, arithmetic and copies ran while one was open for 49% of the time, Pallas kernels for 0%

profile of v3, /device:TPU:4, one launch (start us, length us, event | category | flops | bytes accessed | tf_op | source)
XLA Modules:
  0.0 471.6 jit_solution(11958535480723115038)
XLA Ops:
  0.0 1.0 fusion.13
  4.4 1.2 reduce-window.6
  11.3 7.5 %all-to-all-start = ((f32[4,1,64]{2,1,0:T(1,128)}), f32[4,1,64]{2,1,0:T(1,128)S(1)}, u32[]{:S(2)}, u32[]{:S(2)}) async-start(f32[4,1,64]{2,1,0:T(1,128)} %convert_element_type.76), calls=%async_computation | async-start | bytes 4096 | tf_op jit(solution)/shard_map/all_to_all | solution.py:84
  20.3 1.3 collective-permute-start.12
  22.1 1.2 fusion.36
  23.3 2.5 slice.113
  25.8 1.4 collective-permute-start.3
  28.0 1.3 collective-permute-start.8
  30.6 2.0 collective-permute-start.13
  32.6 5.5 %all-to-all-start.1 = ((f32[4,64,512]{2,1,0:T(8,128)}), f32[4,64,512]{2,1,0:T(8,128)S(1)}, u32[]{:S(2)}, u32[]{:S(2)}) async-start(f32[4,64,512]{2,1,0:T(8,128)} %fusion.36), calls=%async_computation.1 | async-start | bytes 1048576 | tf_op jit(solution)/shard_map/all_to_all | solution.py:81
  38.1 1.5 bitcast_convert_fusion
  39.7 5.5 %all-to-all-done.1 = f32[4,64,512]{2,1,0:T(8,128)S(1)} async-done(((f32[4,64,512]{2,1,0:T(8,128)}), f32[4,64,512]{2,1,0:T(8,128)S(1)}, u32[]{:S(2)}, u32[]{:S(2)}) %all-to-all-start.1) | async-done | bytes 524320 | tf_op jit(solution)/shard_map/all_to_all | solution.py:81
  46.0 1.2 copy.182
  47.3 1.0 add.223
  48.3 1.3 collective-permute-start.4
  49.6 1.1 add.228
  50.7 4.6 collective-permute-start.9
  55.2 1.1 add.233
  56.3 1.3 collective-permute-start.14
  57.6 2.5 multiply_add_fusion
  60.9 3.8 collective-permute-done.14
  64.7 2.6 copy.183
  67.4 10.4 %all-to-all-start.2 = ((f32[8,320,2,256]{3,1,2,0:T(8,128)}), f32[8,320,2,256]{3,1,2,0:T(8,128)}, u32[]{:S(2)}, u32[]{:S(2)}) async-start(f32[8,320,2,256]{3,1,2,0:T(8,128)} %copy.183), calls=%async_computation.2 | async-start | bytes 10485760 | tf_op jit(solution)/shard_map/all_to_all | solution.py:102
  77.9 14.0 %copy.168 = f32[10,1,256,5,1,256]{5,3,2,0,4,1:T(8,128)} copy(bf16[10,1,256,5,1,256]{5,2,4,3,1,0:T(8,128)(2,1)} %param.13) | data formatting | bytes 19660800 | tf_op jit(solution)/shard_map/convert_element_type | solution.py:114
  92.6 15.8 %copy.203 = f32[320,8,5,256]{3,1,2,0:T(8,128)} copy(f32[320,8,5,256]{3,2,1,0:T(8,128)} %bitcast.200) | data formatting | bytes 26214400
  108.7 6.4 %broadcast_in_dim.83 = f32[2560,5,256]{0,2,1:T(8,128)} broadcast(f32[2560,5]{0,1:T(8,128)S(1)} %bitcast.223), dimensions={0,1} | broadcast | bytes 13158400 | tf_op jit(solution)/shard_map/broadcast_in_dim | solution.py:127
  115.1 14.0 %copy.169 = f32[2560,1280]{1,0:T(8,128)} copy(f32[2560,1280]{0,1:T(8,128)} %bitcast.208) | data formatting | bytes 26214400 | tf_op jit(solution)/shard_map/reshape | solution.py:127
  130.7 14.6 %multiply_select_fusion = f32[2560,1280]{1,0:T(8,128)} fusion(f32[2560,1280]{1,0:T(8,128)} %copy.169, f32[2560,1280]{1,0:T(8,128)} %bitcast.202, s32[1280]{0:T(1024)S(1)} %gt.19, s32[2560]{0:T(1024)S(1)} %gt.17), kind=kLoop, calls=%fused_computation.7 | loop fusion | flops 9830400 | bytes 39336960 | tf_op jit(solution)/shard_map/jit(_where)/select_n | solution.py:128
  145.3 2.2 constant_dynamic-slice_fusion.9
  147.5 47.2 %all-to-all-done.2 = f32[8,320,2,256]{3,1,2,0:T(8,128)} async-done(((f32[8,320,2,256]{3,1,2,0:T(8,128)}), f32[8,320,2,256]{3,1,2,0:T(8,128)}, u32[]{:S(2)}, u32[]{:S(2)}) %all-to-all-start.2) | async-done | bytes 5242912 | tf_op jit(solution)/shard_map/all_to_all | solution.py:102
  194.8 2.9 reduce_sum.38
  197.8 2.8 broadcast_in_dim.92
  200.7 4.6 all-to-all-start.3
  205.9 1.8 fusion.28
  207.7 1.8 fusion.26
  209.5 1.8 fusion.24
  211.3 1.8 fusion.22
  215.4 5.0 %gather_fusion = f32[512]{0:T(512)S(1)} fusion(f32[512,512]{0,1:T(8,128)S(1)} %get-tuple-element.90, s32[512]{0:T(512)S(1)} %bitcast.215), kind=kCustom, calls=%fused_computation | custom fusion | bytes 8192 | tf_op jit(solution)/shard_map/jit(diagonal)/cond/branch_0_fun/gather | solution.py:27
  220.8 11.7 %cholesky.130 = f32[128,128]{1,0:T(8,128)S(1)} custom-call(f32[128,128]{1,0:T(8,128)S(1)} %cholesky.194), custom_call_target="Cholesky" | custom-call | tf_op jit(solution)/shard_map/jit(cholesky)/cholesky | solution.py:29
  232.6 9.8 %custom-call.15 = f32[1,128,128]{1,2,0:T(8,128)S(1)} custom-call(f32[1,128,128]{2,1,0:T(8,128)S(1)} %get-tuple-element.101), custom_call_target="InvertDiagBlocksLowerTriangular" | custom-call | tf_op jit(solution)/shard_map/jit(cholesky)/cholesky | solution.py:29
  242.9 11.7 %cholesky.147 = f32[128,128]{1,0:T(8,128)S(1)} custom-call(f32[128,128]{1,0:T(8,128)S(1)} %convolution_subtract_fusion.5), custom_call_target="Cholesky" | custom-call | tf_op jit(solution)/shard_map/jit(cholesky)/cholesky | solution.py:29
  257.3 3.9 while.6
  257.9 1.3 bitcast_dynamic-update-slice_fusion.4
  259.9 1.3 bitcast_dynamic-update-slice_fusion.4
  261.2 19.8 %custom-call.16 = f32[2,128,128]{1,2,0:T(8,128)S(1)} custom-call(f32[2,128,128]{2,1,0:T(8,128)S(1)} %get-tuple-element.57), custom_call_target="InvertDiagBlocksLowerTriangular" | custom-call | tf_op jit(solution)/shard_map/jit(_solve_triangular)/triangular_solve | solution.py:15
  283.2 11.7 %cholesky.164 = f32[128,128]{1,0:T(8,128)S(1)} custom-call(f32[128,128]{1,0:T(8,128)S(1)} %cholesky.197), custom_call_target="Cholesky" | custom-call | tf_op jit(solution)/shard_map/jit(cholesky)/cholesky | solution.py:33
  295.0 9.8 %custom-call.17 = f32[1,128,128]{1,2,0:T(8,128)S(1)} custom-call(f32[1,128,128]{2,1,0:T(8,128)S(1)} %get-tuple-element.97), custom_call_target="InvertDiagBlocksLowerTriangular" | custom-call | tf_op jit(solution)/shard_map/jit(cholesky)/cholesky | solution.py:33
  305.3 11.7 %cholesky.181 = f32[128,128]{1,0:T(8,128)S(1)} custom-call(f32[128,128]{1,0:T(8,128)S(1)} %convolution_subtract_fusion.4), custom_call_target="Cholesky" | custom-call | tf_op jit(solution)/shard_map/jit(cholesky)/cholesky | solution.py:33
  319.7 3.9 while.7
  320.3 1.3 bitcast_dynamic-update-slice_fusion.5
  322.2 1.3 bitcast_dynamic-update-slice_fusion.5
  323.6 19.9 %custom-call.18 = f32[2,128,128]{1,2,0:T(8,128)S(1)} custom-call(f32[2,128,128]{2,1,0:T(8,128)S(1)} %get-tuple-element.58), custom_call_target="InvertDiagBlocksLowerTriangular" | custom-call | tf_op jit(solution)/shard_map/jit(_solve_triangular)/triangular_solve | solution.py:15
  344.5 2.8 copy.185
  347.3 2.4 fusion.2
  349.7 2.3 convolution_subtract_fusion
  352.0 2.4 convolution_bitcast_fusion
  355.0 2.0 copy.210
  357.2 3.8 collective-permute-start.15
  362.0 5.9 %copy.192 = f32[2560,2,256]{0,2,1:T(8,128)} copy(f32[2560,2,256]{2,0,1:T(8,128)} %copy-done) | data formatting | bytes 10485760 | tf_op jit(solution)/shard_map/scatter | solution.py:149
  367.9 51.2 %collective-permute-done.15 = f32[5,256,2,256]{3,2,1,0:T(2,128)} collective-permute-done((f32[5,256,2,256]{3,2,1,0:T(2,128)S(1)}, f32[5,256,2,256]{3,2,1,0:T(2,128)}, u32[]{:S(2)}, u32[]{:S(2)}) %collective-permute-start.15) | collective-permute-done | bytes 2621472 | tf_op jit(solution)/shard_map/ppermute | solution.py:161
  419.1 2.1 copy.206
  421.2 27.0 %fusion = f32[2560,1280]{1,0:T(8,128)} fusion(f32[2560,1280]{1,0:T(8,128)} %fusion.22, f32[2560,512]{0,1:T(8,128)S(1)} %bitcast.214, f32[1280,512]{1,0:T(8,128)S(1)} %bitcast.219, s32[1280]{0:T(1024)S(1)} %gt.19, s32[2560]{0:T(1024)S(1)} %gt.17), kind=kOutput, calls=%fused_computation.6 | convolution fusion | flops 10076160000 | bytes 34094080 | tf_op jit(solution)/shard_map/dot_general | solution.py:165
  448.3 4.4 fusion.1
  452.6 18.5 %reshape.279 = f32[10,1,256,5,1,256]{5,4,3,2,1,0:T(1,128)} reshape(f32[2560,1280]{1,0:T(8,128)} %fusion.1) | data formatting | bytes 26214400 | tf_op jit(solution)/shard_map/reshape | solution.py:169
  (156 shorter events, 30.7 us)
Async XLA Ops:
  0.0 21.7 %copy-start.3 = (f32[1,256,2,256]{3,2,1,0:T(2,128)S(1)}, f32[1,256,2,256]{3,2,1,0:T(2,128)}, u32[]{:S(2)}) copy-start(f32[1,256,2,256]{3,2,1,0:T(2,128)} %param.14) | copy-start | bytes 1572868
  1.0 5.8 %collective-permute-start.10 = (f32[256,256]{1,0:T(8,128)S(1)}, f32[256,256]{1,0:T(8,128)S(1)}, u32[]{:S(2)}, u32[]{:S(2)}) collective-permute-start(f32[256,256]{1,0:T(8,128)S(1)} %get-tuple-element.87), channel_id=1, source_target_pairs={{9,10}} | collective-permute-start | bytes 786440 | tf_op jit(solution)/shard_map/ppermute | solution.py:65
  1.7 5.1 %collective-permute-start = (f32[256,256]{1,0:T(8,128)S(1)}, f32[256,256]{1,0:T(8,128)S(1)}, u32[]{:S(2)}, u32[]{:S(2)}) collective-permute-start(f32[256,256]{1,0:T(8,128)S(1)} %get-tuple-element.89), channel_id=1, source_target_pairs={{0,1}} | collective-permute-start | bytes 786440 | tf_op jit(solution)/shard_map/ppermute | solution.py:65
  2.4 4.4 collective-permute-start.5
  7.8 11.0 %collective-permute-start.1 = (f32[256,256]{1,0:T(8,128)S(1)}, f32[256,256]{1,0:T(8,128)S(1)}, u32[]{:S(2)}, u32[]{:S(2)}) collective-permute-start(f32[256,256]{1,0:T(8,128)S(1)} %get-tuple-element.85), channel_id=1, source_target_pairs={{0,2},{1,3}} | collective-permute-start | bytes 786440 | tf_op jit(solution)/shard_map/ppermute | solution.py:65
  8.5 11.0 %collective-permute-start.6 = (f32[256,256]{1,0:T(8,128)S(1)}, f32[256,256]{1,0:T(8,128)S(1)}, u32[]{:S(2)}, u32[]{:S(2)}) collective-permute-start(f32[256,256]{1,0:T(8,128)S(1)} %get-tuple-element.86), channel_id=1, source_target_pairs={{8,10},{9,11}} | collective-permute-start | bytes 786440 | tf_op jit(solution)/shard_map/ppermute | solution.py:65
  9.2 11.1 %collective-permute-start.11 = (f32[256,256]{1,0:T(8,128)S(1)}, f32[256,256]{1,0:T(8,128)S(1)}, u32[]{:S(2)}, u32[]{:S(2)}) collective-permute-start(f32[256,256]{1,0:T(8,128)S(1)} %get-tuple-element.84), channel_id=1, source_target_pairs={{9,11},{10,12}} | collective-permute-start | bytes 786440 | tf_op jit(solution)/shard_map/ppermute | solution.py:65
  11.3 21.2 %all-to-all-start = ((f32[4,1,64]{2,1,0:T(1,128)}), f32[4,1,64]{2,1,0:T(1,128)S(1)}, u32[]{:S(2)}, u32[]{:S(2)}) async-start(f32[4,1,64]{2,1,0:T(1,128)} %convert_element_type.76), calls=%async_computation | async-start | bytes 4096 | tf_op jit(solution)/shard_map/all_to_all | solution.py:84
  18.9 6.9 %collective-permute-start.2 = (f32[256,256]{1,0:T(8,128)S(1)}, f32[256,256]{1,0:T(8,128)S(1)}, u32[]{:S(2)}, u32[]{:S(2)}) collective-permute-start(f32[256,256]{1,0:T(8,128)S(1)} %add.221), channel_id=1, source_target_pairs={{0,4},{1,5},{2,6},{3,7}} | collective-permute-start | bytes 786440 | tf_op jit(solution)/shard_map/ppermute | solution.py:65
  19.6 7.6 %collective-permute-start.7 = (f32[256,256]{1,0:T(8,128)S(1)}, f32[256,256]{1,0:T(8,128)S(1)}, u32[]{:S(2)}, u32[]{:S(2)}) collective-permute-start(f32[256,256]{1,0:T(8,128)S(1)} %add.226), channel_id=1, source_target_pairs={{8,12},{9,13},{10,14},{11,15}} | collective-permute-start | bytes 786440 | tf_op jit(solution)/shard_map/ppermute | solution.py:65
  20.3 9.5 %collective-permute-start.12 = (f32[256,256]{1,0:T(8,128)S(1)}, f32[256,256]{1,0:T(8,128)S(1)}, u32[]{:S(2)}, u32[]{:S(2)}) collective-permute-start(f32[256,256]{1,0:T(8,128)S(1)} %add.231), channel_id=1, source_target_pairs={{9,13},{10,14},{11,15},{12,16}} | collective-permute-start | bytes 786440 | tf_op jit(solution)/shard_map/ppermute | solution.py:65
  25.8 21.4 %collective-permute-start.3 = (f32[256,256]{1,0:T(8,128)S(1)}, f32[256,256]{1,0:T(8,128)}, u32[]{:S(2)}, u32[]{:S(2)}) collective-permute-start(f32[256,256]{1,0:T(8,128)S(1)} %add.222), channel_id=1, source_target_pairs={{0,8},{1,9},{2,10},{3,11},{4,12},{5,13},{6,14},{7,15}} | collective-permute-start | bytes 786440 | tf_op jit(solution)/shard_map/ppermute | solution.py:65
  28.0 21.6 %collective-permute-start.8 = (f32[256,256]{1,0:T(8,128)}, f32[256,256]{1,0:T(8,128)}, u32[]{:S(2)}, u32[]{:S(2)}) collective-permute-start(f32[256,256]{1,0:T(8,128)} %add.227), channel_id=1, source_target_pairs={{8,16},{9,17},{10,18},{11,19},{12,20},{13,21},{14,22},{15,23}} | collective-permute-start | bytes 786440 | tf_op jit(solution)/shard_map/ppermute | solution.py:65
  30.6 24.7 %collective-permute-start.13 = (f32[256,256]{1,0:T(8,128)}, f32[256,256]{1,0:T(8,128)}, u32[]{:S(2)}, u32[]{:S(2)}) collective-permute-start(f32[256,256]{1,0:T(8,128)} %add.232), channel_id=1, source_target_pairs={{9,17},{10,18},{11,19},{12,20},{13,21},{14,22},{15,23},{16,24}} | collective-permute-start | bytes 786440 | tf_op jit(solution)/shard_map/ppermute | solution.py:65
  32.6 12.7 %all-to-all-start.1 = ((f32[4,64,512]{2,1,0:T(8,128)}), f32[4,64,512]{2,1,0:T(8,128)S(1)}, u32[]{:S(2)}, u32[]{:S(2)}) async-start(f32[4,64,512]{2,1,0:T(8,128)} %fusion.36), calls=%async_computation.1 | async-start | bytes 1048576 | tf_op jit(solution)/shard_map/all_to_all | solution.py:81
  45.2 0.8 copy-start.2
  48.3 11.9 %collective-permute-start.4 = (f32[256,256]{1,0:T(8,128)S(1)}, f32[256,256]{1,0:T(8,128)S(1)}, u32[]{:S(2)}, u32[]{:S(2)}) collective-permute-start(f32[256,256]{1,0:T(8,128)S(1)} %add.223), channel_id=1, source_target_pairs={{0,16},{1,17},{2,18},{3,19},{4,20},{5,21},{6,22},{7,23},{8,24},{9,... | collective-permute-start | bytes 786440 | tf_op jit(solution)/shard_map/ppermute | solution.py:65
  50.7 10.2 %collective-permute-start.9 = (f32[256,256]{1,0:T(8,128)S(1)}, f32[256,256]{1,0:T(8,128)S(1)}, u32[]{:S(2)}, u32[]{:S(2)}) collective-permute-start(f32[256,256]{1,0:T(8,128)S(1)} %add.228), channel_id=1, source_target_pairs={{8,24},{9,25},{10,26},{11,27},{12,28},{13,29},{14,30},{15,31},{16,... | collective-permute-start | bytes 786440 | tf_op jit(solution)/shard_map/ppermute | solution.py:65
  56.3 8.4 %collective-permute-start.14 = (f32[256,256]{1,0:T(8,128)S(1)}, f32[256,256]{1,0:T(8,128)S(1)}, u32[]{:S(2)}, u32[]{:S(2)}) collective-permute-start(f32[256,256]{1,0:T(8,128)S(1)} %add.233), channel_id=1, source_target_pairs={{9,25},{10,26},{11,27},{12,28},{13,29},{14,30},{15,31},{16,0},{17,... | collective-permute-start | bytes 786440 | tf_op jit(solution)/shard_map/ppermute | solution.py:65
  67.4 127.4 %all-to-all-start.2 = ((f32[8,320,2,256]{3,1,2,0:T(8,128)}), f32[8,320,2,256]{3,1,2,0:T(8,128)}, u32[]{:S(2)}, u32[]{:S(2)}) async-start(f32[8,320,2,256]{3,1,2,0:T(8,128)} %copy.183), calls=%async_computation.2 | async-start | bytes 10485760 | tf_op jit(solution)/shard_map/all_to_all | solution.py:102
  77.8 14.0 %copy-start.4 = (s32[40,40]{1,0:T(8,128)S(1)}, s32[40,40]{1,0:T(8,128)}, u32[]{:S(2)}) copy-start(s32[40,40]{1,0:T(8,128)} %param.18) | copy-start | bytes 19204
  200.7 143.8 %all-to-all-start.3 = ((f32[8,320,2,256]{3,1,2,0:T(8,128)}), f32[8,320,2,256]{3,1,2,0:T(8,128)}, u32[]{:S(2)}, u32[]{:S(2)}) async-start(f32[8,320,2,256]{3,1,2,0:T(8,128)} %broadcast_in_dim.92), calls=%async_computation.3 | async-start | bytes 10485760 | tf_op jit(solution)/shard_map/all_to_all | solution.py:107
  354.8 2.4 copy-start
  357.2 61.9 %collective-permute-start.15 = (f32[5,256,2,256]{3,2,1,0:T(2,128)S(1)}, f32[5,256,2,256]{3,2,1,0:T(2,128)}, u32[]{:S(2)}, u32[]{:S(2)}) collective-permute-start(f32[5,256,2,256]{3,2,1,0:T(2,128)S(1)} %bitcast.220), channel_id=1, source_target_pairs={{0,0},{1,8},{2,16},{3,24},{4,4},{5,12},{6,20},{7,28},{8,1},{9,9},{... | collective-permute-start | bytes 7864328 | tf_op jit(solution)/shard_map/ppermute | solution.py:161
  367.9 53.3 %copy-start.1 = (f32[2560,2,256]{0,2,1:T(8,128)S(1)}, f32[2560,2,256]{0,2,1:T(8,128)}, u32[]{:S(2)}) copy-start(f32[2560,2,256]{0,2,1:T(8,128)} %copy.192) | copy-start | bytes 15728644
  419.1 29.2 %slice-start = ((s8[5242880]{0:T(1024)(128)(4,1)}), s8[4194304]{0:T(1024)(128)(4,1)S(1)}, s32[]{:S(2)}) async-start(s8[5242880]{0:T(1024)(128)(4,1)} %bitcast.210), calls=%async_computation.4 | async-start | bytes 8388608
  421.2 27.0 %slice-start.1 = ((s8[5242880]{0:T(1024)(128)(4,1)}), s8[1048576]{0:T(1024)(128)(4,1)S(1)}, s32[]{:S(2)}) async-start(s8[5242880]{0:T(1024)(128)(4,1)} %bitcast.210), calls=%async_computation.5 | async-start | bytes 2097152
